TPU v7x, 512 devices: a whole 4x4x16 slice. The times are simulated.
512 devices in a mesh: seq: 128 (over z, x, core), fsdp: 4 (over y).
Axes of the slice: x: 4, y: 4, z: 16, core: 2. Of those that a mesh axis runs over, the one named last changes fastest.
Arguments:
- query_key: bfloat16 [131072, 3072], P(('seq', 'fsdp')), may hold values from -48 to 48
- values: bfloat16 [131072, 3072], P(('seq', 'fsdp')), may hold values from -6 to 6
- cluster_ids: int32 [24, 1024], replicated, may hold values from 0 to 127, as said below
Outputs:
- attended: bfloat16 [131072, 3072], P(('seq', 'fsdp'))
Inputs may be any that keep to these rules, and one draw needn't show every extreme that they name: `cluster_ids`: for every head and cluster at most 10 blocks name that cluster, and for every head some cluster is named by exactly 10 blocks. Among the (head, block) pairs of one group of 6 consecutive heads and one run of 8 blocks starting at a multiple of 8, no cluster is named more than 1 times, and some cluster exactly 1 times; the blocks of one such run name distinct clusters for each head.
All inputs are finite; a program needn't handle non-finite values.
Results may differ from a plain program's by a relative error of at most 0.0027.
Values may be sent and summed in bfloat16 or wider, within the bound.
No kernel may reach another device: no remote copies, remote signals or barrier semaphores. Data moves between devices by JAX's collectives and lax.ppermute only.
A program may use at most 64 MiB of HBM per device.

v0:
```python
import math

import jax
import jax.numpy as jnp
from jax import lax
from jax.sharding import PartitionSpec as P

BLK = 128


masked_score = -1e30


def by_index(source_table, row_index):
    padded = jnp.concatenate(
        [source_table, jnp.zeros((1,) + source_table.shape[1:], source_table.dtype)], axis=0
    )
    return padded[row_index]


def attend_group(key_rows, value_rows, positions, alive_rows, score_scale):
    scores = jnp.dot(key_rows, key_rows.T, preferred_element_type=jnp.float32) * score_scale
    allowed = alive_rows[None, :] & (positions[None, :] <= positions[:, None])
    scores = jnp.where(allowed, scores, masked_score)
    row_peak = jnp.max(scores, axis=1, keepdims=True)
    weights = jnp.where(allowed, jnp.exp(scores - row_peak), 0.0)
    row_total = jnp.where(alive_rows[:, None], jnp.sum(weights, axis=1, keepdims=True), 1.0)
    weighted = jnp.dot(weights.astype(jnp.bfloat16), value_rows, preferred_element_type=jnp.float32)
    return (weighted / row_total).astype(jnp.bfloat16)


def shards(query_key, values, cluster_ids):
    seq_count = lax.axis_size("seq")
    group_count = lax.axis_size("fsdp")
    seq_index = lax.axis_index("seq")
    group_index = lax.axis_index("fsdp")
    heads_all = cluster_ids.shape[0]
    group_heads = heads_all // group_count
    head_dim = query_key.shape[1] // heads_all
    tok_rows = query_key.shape[0]
    shard_blocks = group_count * tok_rows // BLK
    all_blocks = cluster_ids.shape[1]
    item_count = group_heads * shard_blocks
    slot_count = max(1, item_count // seq_count)
    capacity = shard_blocks + min(shard_blocks // 4, seq_count - shard_blocks)
    group_rows = capacity * BLK
    send_rows = seq_count * slot_count
    score_scale = 1.0 / math.sqrt(head_dim)
    keys_local, values_local = (
        lax.all_to_all(query_key, "fsdp", split_axis=1, concat_axis=0, tiled=True),
        lax.all_to_all(values, "fsdp", split_axis=1, concat_axis=0, tiled=True),
    )

    def into_items(block_data):
        shaped = block_data.reshape(shard_blocks, BLK, group_heads, head_dim)
        return jnp.transpose(shaped, (2, 0, 1, 3)).reshape(item_count, BLK, head_dim)

    key_items = into_items(keys_local)
    value_items = into_items(values_local)
    group_ids = lax.dynamic_slice_in_dim(cluster_ids, group_index * group_heads, group_heads, 0)
    by_source = jnp.transpose(
        group_ids.reshape(group_heads, seq_count, shard_blocks), (1, 0, 2)
    ).reshape(seq_count, item_count)
    own_dest = lax.dynamic_index_in_dim(by_source, seq_index, 0, keepdims=False)
    item_ids = jnp.arange(item_count, dtype=jnp.int32)
    earlier = (own_dest[None, :] == own_dest[:, None]) & (item_ids[None, :] < item_ids[:, None])
    own_pos = own_dest * slot_count + jnp.sum(earlier.astype(jnp.int32), axis=1)
    row_ids = jnp.arange(send_rows, dtype=jnp.int32)
    slot_match = own_pos[None, :] == row_ids[:, None]
    send_pick = jnp.sum(jnp.where(slot_match, item_ids[None, :], 0), axis=1) + item_count * (
        1 - jnp.any(slot_match, axis=1).astype(jnp.int32)
    )
    received_mask = (by_source == seq_index).astype(jnp.int32)
    recv_pos = (
        jnp.arange(seq_count, dtype=jnp.int32)[:, None] * slot_count
        + jnp.cumsum(received_mask, axis=1)
        - received_mask
    )
    recv_by_head = jnp.transpose(
        recv_pos.reshape(seq_count, group_heads, shard_blocks), (1, 0, 2)
    ).reshape(group_heads * all_blocks)
    owned_mask = (group_ids == seq_index).astype(jnp.int32)
    ordinal = jnp.cumsum(owned_mask, axis=1) - owned_mask
    target = jnp.where(
        owned_mask > 0, jnp.arange(group_heads, dtype=jnp.int32)[:, None] * capacity + ordinal, -1
    ).reshape(group_heads * all_blocks)
    slot_ids = jnp.arange(group_heads * capacity, dtype=jnp.int32)
    matches = target[None, :] == slot_ids[:, None]
    present = jnp.any(matches, axis=1)
    source_row = jnp.sum(jnp.where(matches, recv_by_head[None, :], 0), axis=1) + send_rows * (
        1 - present.astype(jnp.int32)
    )
    block_ids = jnp.tile(jnp.arange(all_blocks, dtype=jnp.int32), group_heads)
    block_of = jnp.sum(jnp.where(matches, block_ids[None, :], 0), axis=1)
    payload = jnp.concatenate([key_items, value_items], axis=2)
    arrived = lax.all_to_all(
        by_index(payload, send_pick), "seq", split_axis=0, concat_axis=0, tiled=True
    )
    grouped = by_index(arrived, source_row)
    key_grouped = grouped[:, :, :head_dim]
    value_grouped = grouped[:, :, head_dim:]
    positions = (block_of[:, None] * BLK + jnp.arange(BLK, dtype=jnp.int32)[None, :]).reshape(
        group_heads, group_rows
    )
    alive_rows = jnp.repeat(present, BLK).reshape(group_heads, group_rows)

    def one_head(operands):
        key_rows, value_rows, where_at, alive_here = operands
        return attend_group(key_rows, value_rows, where_at, alive_here, score_scale)

    outputs = lax.map(
        one_head,
        (
            key_grouped.reshape(group_heads, group_rows, head_dim),
            value_grouped.reshape(group_heads, group_rows, head_dim),
            positions,
            alive_rows,
        ),
    )
    outputs = outputs.reshape(group_heads * capacity, BLK, head_dim)
    back_match = source_row[None, :] == row_ids[:, None]
    back_pick = jnp.sum(
        jnp.where(back_match, slot_ids[None, :], 0), axis=1
    ) + group_heads * capacity * (1 - jnp.any(back_match, axis=1).astype(jnp.int32))
    returned = lax.all_to_all(
        by_index(outputs, back_pick), "seq", split_axis=0, concat_axis=0, tiled=True
    )
    own_output = by_index(returned, own_pos)
    token_major = jnp.transpose(
        own_output.reshape(group_heads, shard_blocks, BLK, head_dim), (1, 2, 0, 3)
    ).reshape(shard_blocks * BLK, group_heads * head_dim)
    return lax.all_to_all(token_major, "fsdp", split_axis=0, concat_axis=1, tiled=True)


def solution(mesh):
    placed = (P(("seq", "fsdp"), None), P(("seq", "fsdp"), None), P())
    return jax.shard_map(
        shards, mesh=mesh, in_specs=placed, out_specs=P(("seq", "fsdp"), None), check_vma=False
    )
```

profile of v0, /device:TPU:70, one launch (start us, length us, event | category | flops | bytes accessed | tf_op | source)
XLA Modules:
  0.0 763.2 jit_solution(17281788151877645556)
XLA Ops:
  0.0 2.6 copy.60
  2.6 4.6 all-to-all-start.1
  20.4 7.5 all-to-all-done.1
  27.9 3.6 all-to-all-start
  32.5 2.4 copy.61
  34.8 2.5 reshape.236
  39.1 12.1 %all-to-all-done = bf16[256,4,768]{0,2,1:T(8,128)(2,1)S(1)} async-done(((bf16[256,4,768]{0,2,1:T(8,128)(2,1)}), bf16[256,4,768]{0,2,1:T(8,128)(2,1)S(1)}, u32[]{:S(2)}, u32[]{:S(2)}) %all-to-all-start) | async-done | bytes 1572896 | tf_op jit(solution)/shard_map/all_to_all | solution.py:50
  57.3 6.4 gather_fusion
  63.8 19.0 %all-to-all-start.2 = ((bf16[128,128,256]{2,1,0:T(8,128)(2,1)}), bf16[128,128,256]{2,1,0:T(8,128)(2,1)}, u32[]{:S(2)}, u32[]{:S(2)}) async-start(bf16[128,128,256]{2,1,0:T(8,128)(2,1)} %gather_fusion), calls=%async_computation.2 | async-start | bytes 16777216 | tf_op jit(solution)/shard_map/all_to_all | solution.py:96
  83.3 367.0 %all-to-all-done.2 = bf16[128,128,256]{2,1,0:T(8,128)(2,1)} async-done(((bf16[128,128,256]{2,1,0:T(8,128)(2,1)}), bf16[128,128,256]{2,1,0:T(8,128)(2,1)}, u32[]{:S(2)}, u32[]{:S(2)}) %all-to-all-start.2) | async-done | bytes 8388640 | tf_op jit(solution)/shard_map/all_to_all | solution.py:96
  450.3 7.7 %concatenate.17 = bf16[129,128,256]{2,1,0:T(8,128)(2,1)} pad(bf16[128,128,256]{2,1,0:T(8,128)(2,1)} %all-to-all-done.2, bf16[]{:T(256)} %constant.34.clone.1), padding=0_1x0_0x0_0 | pad | bytes 16842754 | tf_op jit(solution)/shard_map/concatenate | solution.py:15
  458.1 6.1 gather_fusion.1
  464.2 4.6 fusion.40
  468.7 54.8 %while.10 = (s32[]{:T(128)}, bf16[6,1280,128]{2,1,0:T(8,128)(2,1)S(1)}, pred[6,1280]{1,0:T(8,128)(4,1)S(1)}, s32[6,1280]{1,0:T(8,128)S(1)}, bf16[6,1280,128]{2,1...) while((s32[]{:T(128)}, bf16[6,1280,128]{2,1,0:T(8,128)(2,1)S(1)}, ...), condition=%wide.region_12.13_spmd, body=%wide.region_9.12_spmd.sunk | while | flops 863763200 | bytes 20744788 | solution.py:111
  468.8 3.4 fusion.48
  474.5 3.3 fusion.50
  477.9 3.4 fusion.48
  483.7 3.3 fusion.50
  487.1 3.4 fusion.48
  492.8 3.3 fusion.50
  496.2 3.4 fusion.48
  501.9 3.3 fusion.50
  505.3 3.4 fusion.48
  511.1 3.3 fusion.50
  514.5 3.4 fusion.48
  520.2 3.3 fusion.50
  526.5 3.0 gather_fusion.2
  529.5 9.2 %all-to-all-start.3 = ((bf16[128,128,128]{2,1,0:T(8,128)(2,1)}), bf16[128,128,128]{2,1,0:T(8,128)(2,1)}, u32[]{:S(2)}, u32[]{:S(2)}) async-start(bf16[128,128,128]{2,1,0:T(8,128)(2,1)} %gather_fusion.2), calls=%async_computation.3 | async-start | bytes 8388608 | tf_op jit(solution)/shard_map/all_to_all | solution.py:125
  538.8 188.1 %all-to-all-done.3 = bf16[128,128,128]{2,1,0:T(8,128)(2,1)} async-done(((bf16[128,128,128]{2,1,0:T(8,128)(2,1)}), bf16[128,128,128]{2,1,0:T(8,128)(2,1)}, u32[]{:S(2)}, u32[]{:S(2)}) %all-to-all-start.3) | async-done | bytes 4194336 | tf_op jit(solution)/shard_map/all_to_all | solution.py:125
  726.9 5.7 concatenate.19
  732.6 3.0 gather_fusion.3
  737.9 23.6 %all_to_all.61 = bf16[4,256,768]{1,2,0:T(8,128)(2,1)S(1)} all-to-all(bf16[4,256,768]{1,2,0:T(8,128)(2,1)S(1)} %copy.67), channel_id=1, replica_groups=mesh['seq'=128,'fsdp'=4] {'fsdp'}, dimensions={0} | all-to-all | bytes 3145728 | tf_op jit(solution)/shard_map/all_to_all | solution.py:132
  (89 shorter events, 43.7 us)
Async XLA Ops:
  2.6 15.8 %copy-start.1 = (bf16[256,3072]{1,0:T(8,128)(2,1)S(1)}, bf16[256,3072]{1,0:T(8,128)(2,1)}, u32[]{:S(2)}) copy-start(bf16[256,3072]{1,0:T(8,128)(2,1)} %param.5) | copy-start | bytes 4718596
  2.6 25.3 %all-to-all-start.1 = ((bf16[256,4,768]{0,2,1:T(8,128)(2,1)}), bf16[256,4,768]{0,2,1:T(8,128)(2,1)S(1)}, u32[]{:S(2)}, u32[]{:S(2)}) async-start(bf16[256,4,768]{0,2,1:T(8,128)(2,1)} %bitcast.10), calls=%async_computation.1 | async-start | bytes 3145728 | tf_op jit(solution)/shard_map/all_to_all | solution.py:51
  17.1 2.9 copy-start.2
  17.1 3.0 copy-start.3
  17.1 14.3 %copy-start.4 = (s32[6144]{0:T(1024)S(1)}, s32[6144]{0:T(1024)}, u32[]{:S(2)}) copy-start(s32[6144]{0:T(1024)} %broadcast_in_dim.110) | copy-start | bytes 73732
  27.9 23.4 %all-to-all-start = ((bf16[256,4,768]{0,2,1:T(8,128)(2,1)}), bf16[256,4,768]{0,2,1:T(8,128)(2,1)S(1)}, u32[]{:S(2)}, u32[]{:S(2)}) async-start(bf16[256,4,768]{0,2,1:T(8,128)(2,1)} %bitcast.6), calls=%async_computation | async-start | bytes 3145728 | tf_op jit(solution)/shard_map/all_to_all | solution.py:50
  63.8 386.6 %all-to-all-start.2 = ((bf16[128,128,256]{2,1,0:T(8,128)(2,1)}), bf16[128,128,256]{2,1,0:T(8,128)(2,1)}, u32[]{:S(2)}, u32[]{:S(2)}) async-start(bf16[128,128,256]{2,1,0:T(8,128)(2,1)} %gather_fusion), calls=%async_computation.2 | async-start | bytes 16777216 | tf_op jit(solution)/shard_map/all_to_all | solution.py:96
  523.5 1.3 copy-start
  529.5 197.4 %all-to-all-start.3 = ((bf16[128,128,128]{2,1,0:T(8,128)(2,1)}), bf16[128,128,128]{2,1,0:T(8,128)(2,1)}, u32[]{:S(2)}, u32[]{:S(2)}) async-start(bf16[128,128,128]{2,1,0:T(8,128)(2,1)} %gather_fusion.2), calls=%async_computation.3 | async-start | bytes 8388608 | tf_op jit(solution)/shard_map/all_to_all | solution.py:125
where the time goes:
time: 765 us; the launch traced here: 763 us
  waiting for transfers between devices  575 us (75%)
  local copies, waits for them, and re-layouts  64.2 us (8%)
  matrix products  40.3 us (5%)
  starting transfers between devices  36.4 us (5%)
  other arithmetic  23.6 us (3%)
  blocking collectives  23.6 us (3%)
    all_to_all x1, waiting for transfers between devices, shards(): lax.all_to_all(by_index(payload, send_pick), 'seq', split_axis=0, concat_...  367 us
    all_to_all x1, waiting for transfers between devices, shards(): lax.all_to_all(by_index(outputs, back_pick), 'seq', split_axis=0, concat_...  188 us
    all_to_all x1, blocking collectives, shards(): lax.all_to_all(token_major, 'fsdp', split_axis=0, concat_axis=1, tiled=True)  23.6 us
    dot_general x6, matrix products, attend_group(): jnp.dot(key_rows, key_rows.T, preferred_element_type=jnp.float32)  20.3 us
    dot_general x6, matrix products, attend_group(): jnp.dot(weights.astype(jnp.bfloat16), value_rows, preferred_element_type=...  20 us
    all_to_all x1, starting transfers between devices, shards(): lax.all_to_all(by_index(payload, send_pick), 'seq', split_axis=0, concat_...  19 us
    gather x4, local copies, waits for them, and re-layouts, by_index(): return padded[row_index]  18.6 us
  transfers between devices with their start and end apart: 4, of which 4 were waited for; matrix products, arithmetic and copies ran while one was open for 3% of the time, Pallas kernels for 0%

commit v1 on v0

--- a/solution.py
+++ b/solution.py
@@ -18,15 +18,26 @@
     return padded[row_index]
 
 
-def attend_group(key_rows, value_rows, positions, alive_rows, score_scale):
-    scores = jnp.dot(key_rows, key_rows.T, preferred_element_type=jnp.float32) * score_scale
-    allowed = alive_rows[None, :] & (positions[None, :] <= positions[:, None])
+def softmax_group(key_rows, positions, alive_rows, score_scale):
+    half = BLK // 2
+    blocks = key_rows.shape[0] // BLK
+
+    def by_half(rows):
+        shaped = rows.reshape((blocks, 2, half) + rows.shape[1:])
+        return jnp.swapaxes(shaped, 0, 1).reshape(rows.shape)
+
+    query_rows = by_half(key_rows)
+    query_positions = by_half(positions)
+    query_alive = by_half(alive_rows)
+    scores = jnp.dot(query_rows, key_rows.T, preferred_element_type=jnp.float32) * score_scale
+    allowed = alive_rows[None, :] & (positions[None, :] <= query_positions[:, None])
     scores = jnp.where(allowed, scores, masked_score)
     row_peak = jnp.max(scores, axis=1, keepdims=True)
     weights = jnp.where(allowed, jnp.exp(scores - row_peak), 0.0)
-    row_total = jnp.where(alive_rows[:, None], jnp.sum(weights, axis=1, keepdims=True), 1.0)
-    weighted = jnp.dot(weights.astype(jnp.bfloat16), value_rows, preferred_element_type=jnp.float32)
-    return (weighted / row_total).astype(jnp.bfloat16)
+    row_total = jnp.where(query_alive[:, None], jnp.sum(weights, axis=1, keepdims=True), 1.0)
+    weights = weights.astype(jnp.bfloat16).reshape(2, blocks * half, key_rows.shape[0])
+    row_total = row_total.reshape(2, blocks * half, 1)
+    return weights[0], weights[1], row_total[0], row_total[1]
 
 
 def shards(query_key, values, cluster_ids):
@@ -92,44 +103,57 @@
     )
     block_ids = jnp.tile(jnp.arange(all_blocks, dtype=jnp.int32), group_heads)
     block_of = jnp.sum(jnp.where(matches, block_ids[None, :], 0), axis=1)
-    payload = jnp.concatenate([key_items, value_items], axis=2)
-    arrived = lax.all_to_all(
-        by_index(payload, send_pick), "seq", split_axis=0, concat_axis=0, tiled=True
+    arrived_k = lax.all_to_all(
+        by_index(key_items, send_pick), "seq", split_axis=0, concat_axis=0, tiled=True
     )
-    grouped = by_index(arrived, source_row)
-    key_grouped = grouped[:, :, :head_dim]
-    value_grouped = grouped[:, :, head_dim:]
+    arrived_v = lax.all_to_all(
+        by_index(value_items, send_pick), "seq", split_axis=0, concat_axis=0, tiled=True
+    )
+    key_grouped = by_index(arrived_k, source_row)
+    value_grouped = by_index(arrived_v, source_row)
     positions = (block_of[:, None] * BLK + jnp.arange(BLK, dtype=jnp.int32)[None, :]).reshape(
         group_heads, group_rows
     )
     alive_rows = jnp.repeat(present, BLK).reshape(group_heads, group_rows)
 
     def one_head(operands):
-        key_rows, value_rows, where_at, alive_here = operands
-        return attend_group(key_rows, value_rows, where_at, alive_here, score_scale)
+        key_rows, where_at, alive_here = operands
+        return softmax_group(key_rows, where_at, alive_here, score_scale)
 
-    outputs = lax.map(
+    weights_0, weights_1, totals_0, totals_1 = lax.map(
         one_head,
-        (
-            key_grouped.reshape(group_heads, group_rows, head_dim),
-            value_grouped.reshape(group_heads, group_rows, head_dim),
-            positions,
-            alive_rows,
-        ),
+        (key_grouped.reshape(group_heads, group_rows, head_dim), positions, alive_rows),
     )
-    outputs = outputs.reshape(group_heads * capacity, BLK, head_dim)
+    half = BLK // 2
+    value_rows = value_grouped.reshape(group_heads, group_rows, head_dim)
     back_match = source_row[None, :] == row_ids[:, None]
     back_pick = jnp.sum(
         jnp.where(back_match, slot_ids[None, :], 0), axis=1
     ) + group_heads * capacity * (1 - jnp.any(back_match, axis=1).astype(jnp.int32))
-    returned = lax.all_to_all(
-        by_index(outputs, back_pick), "seq", split_axis=0, concat_axis=0, tiled=True
+    pieces = []
+    for part in range(2):
+        part_weights = (weights_0, weights_1)[part]
+        weighted = jnp.einsum(
+            "hqk,hkd->hqd", part_weights, value_rows, preferred_element_type=jnp.float32
+        )
+        part_total = (totals_0, totals_1)[part]
+        outputs = (weighted / part_total).astype(jnp.bfloat16)
+        outputs = outputs.reshape(group_heads * capacity, half, head_dim)
+        returned = lax.all_to_all(
+            by_index(outputs, back_pick), "seq", split_axis=0, concat_axis=0, tiled=True
+        )
+        own_output = by_index(returned, own_pos)
+        token_major = jnp.transpose(
+            own_output.reshape(group_heads, shard_blocks, half, head_dim), (1, 2, 0, 3)
+        ).reshape(shard_blocks * half, group_heads * head_dim)
+        pieces.append(
+            lax.all_to_all(token_major, "fsdp", split_axis=0, concat_axis=1, tiled=True)
+        )
+    own_blocks = tok_rows // BLK
+    joined = jnp.stack(
+        [piece.reshape(own_blocks, half, heads_all * head_dim) for piece in pieces], axis=1
     )
-    own_output = by_index(returned, own_pos)
-    token_major = jnp.transpose(
-        own_output.reshape(group_heads, shard_blocks, BLK, head_dim), (1, 2, 0, 3)
-    ).reshape(shard_blocks * BLK, group_heads * head_dim)
-    return lax.all_to_all(token_major, "fsdp", split_axis=0, concat_axis=1, tiled=True)
+    return joined.reshape(tok_rows, heads_all * head_dim)
 
 
 def solution(mesh):

time: 765 us -> 735 us (0.961)
  the two profiles are of different devices: /device:TPU:70 before, /device:TPU:32 now
where the time goes in v1:
time: 735 us; the launch traced here: 726 us
  waiting for transfers between devices  530 us (72%)
  local copies, waits for them, and re-layouts  83.8 us (11%)
  starting transfers between devices  62.9 us (9%)
  matrix products  25.9 us (4%)
  other arithmetic  22 us (3%)
    all_to_all x2, waiting for transfers between devices, shards(): lax.all_to_all(by_index(outputs, back_pick), 'seq', split_axis=0, concat_...  180 us
    all_to_all x1, waiting for transfers between devices, shards(): lax.all_to_all(by_index(key_items, send_pick), 'seq', split_axis=0, conca...  179 us
    all_to_all x1, waiting for transfers between devices, shards(): lax.all_to_all(by_index(value_items, send_pick), 'seq', split_axis=0, con...  137 us
    gather x8, local copies, waits for them, and re-layouts, by_index(): return padded[row_index]  19.8 us
    all_to_all x1, starting transfers between devices, shards(): lax.all_to_all(by_index(key_items, send_pick), 'seq', split_axis=0, conca...  19.5 us
    all_to_all x2, waiting for transfers between devices, shards(): lax.all_to_all(token_major, 'fsdp', split_axis=0, concat_axis=1, tiled=True)  18.9 us
    concatenate x8, local copies, waits for them, and re-layouts, by_index(): jnp.concatenate([source_table, jnp.zeros((1,) + source_table.shape[1:], s...  18.7 us
    all_to_all x2, starting transfers between devices, shards(): lax.all_to_all(by_index(outputs, back_pick), 'seq', split_axis=0, concat_...  18 us
  transfers between devices with their start and end apart: 8, of which 8 were waited for; matrix products, arithmetic and copies ran while one was open for 14% of the time, Pallas kernels for 0%

profile of v1, /device:TPU:32, one launch (start us, length us, event | category | flops | bytes accessed | tf_op | source)
XLA Modules:
  0.0 725.8 jit_solution(8790920589746454872)
XLA Ops:
  0.0 2.6 copy.104
  2.6 4.6 all-to-all-start
  20.4 7.5 %all-to-all-done = bf16[256,4,768]{0,2,1:T(8,128)(2,1)S(1)} async-done(((bf16[256,4,768]{0,2,1:T(8,128)(2,1)}), bf16[256,4,768]{0,2,1:T(8,128)(2,1)S(1)}, u32[]{:S(2)}, u32[]{:S(2)}) %all-to-all-start) | async-done | bytes 1572896 | tf_op jit(solution)/shard_map/all_to_all | solution.py:61
  27.9 3.6 all-to-all-start.2
  34.8 2.5 reshape.280
  40.7 3.1 gather_fusion
  43.8 7.5 %all-to-all-done.2 = bf16[256,4,768]{0,2,1:T(8,128)(2,1)S(1)} async-done(((bf16[256,4,768]{0,2,1:T(8,128)(2,1)}), bf16[256,4,768]{0,2,1:T(8,128)(2,1)S(1)}, u32[]{:S(2)}, u32[]{:S(2)}) %all-to-all-start.2) | async-done | bytes 1572896 | tf_op jit(solution)/shard_map/all_to_all | solution.py:62
  51.3 19.5 %all-to-all-start.1 = ((bf16[128,128,128]{2,1,0:T(8,128)(2,1)}), bf16[128,128,128]{2,1,0:T(8,128)(2,1)}, u32[]{:S(2)}, u32[]{:S(2)}) async-start(bf16[128,128,128]{2,1,0:T(8,128)(2,1)} %gather_fusion), calls=%async_computation.1 | async-start | bytes 8388608 | tf_op jit(solution)/shard_map/all_to_all | solution.py:106
  76.1 3.1 gather_fusion.2
  79.2 179.2 %all-to-all-done.1 = bf16[128,128,128]{2,1,0:T(8,128)(2,1)} async-done(((bf16[128,128,128]{2,1,0:T(8,128)(2,1)}), bf16[128,128,128]{2,1,0:T(8,128)(2,1)}, u32[]{:S(2)}, u32[]{:S(2)}) %all-to-all-start.1) | async-done | bytes 4194336 | tf_op jit(solution)/shard_map/all_to_all | solution.py:106
  258.4 9.4 %all-to-all-start.3 = ((bf16[128,128,128]{2,1,0:T(8,128)(2,1)}), bf16[128,128,128]{2,1,0:T(8,128)(2,1)}, u32[]{:S(2)}, u32[]{:S(2)}) async-start(bf16[128,128,128]{2,1,0:T(8,128)(2,1)} %gather_fusion.2), calls=%async_computation.3 | async-start | bytes 8388608 | tf_op jit(solution)/shard_map/all_to_all | solution.py:109
  268.3 5.8 concatenate.25
  274.1 3.1 gather_fusion.1
  277.3 41.2 %while.16 = (s32[]{:T(128)}, bf16[6,640,1280]{1,2,0:T(8,128)(2,1)}, bf16[6,640,1280]{1,2,0:T(8,128)(2,1)}, f32[6,640,1]{1,0,2:T(8,128)S(1)}, f32[6,640,1]{1,0,2:...) while((s32[]{:T(128)}, bf16[6,640,1280]{1,2,0:T(8,128)(2,1)}, ...), condition=%wide.region_12.13_spmd, body=%wide.region_9.12_spmd.sunk | while | flops 437451520 | bytes 25025912 | solution.py:123
  279.3 2.4 fusion.30
  286.2 2.4 fusion.30
  293.1 2.4 fusion.30
  299.9 2.4 fusion.30
  306.8 2.4 fusion.30
  318.5 137.1 %all-to-all-done.3 = bf16[128,128,128]{2,1,0:T(8,128)(2,1)} async-done(((bf16[128,128,128]{2,1,0:T(8,128)(2,1)}), bf16[128,128,128]{2,1,0:T(8,128)(2,1)}, u32[]{:S(2)}, u32[]{:S(2)}) %all-to-all-start.3) | async-done | bytes 4194336 | tf_op jit(solution)/shard_map/all_to_all | solution.py:109
  455.5 5.8 concatenate.27
  461.3 3.1 gather_fusion.3
  464.5 7.7 %divide_convert_fusion.1 = bf16[6,640,128]{2,1,0:T(8,128)(2,1)S(1)} fusion(f32[6,640]{1,0:T(8,128)S(1)} %bitcast.151, bf16[6,640,1280]{1,2,0:T(8,128)(2,1)} %get-tuple-element.50, bf16[6,1280,128]{2,1,0:T(8,128)(2,1)S(1)} %bitcast.140), kind=kOutput, calls=%fused_computation.26 | convolution fusion | flops 1259274240 | bytes 12794880 | tf_op jit(solution)/shard_map/hqk,hkd->hqd/dot_general | solution.py:136
  474.5 8.9 %all-to-all-start.4 = ((bf16[128,64,128]{2,1,0:T(8,128)(2,1)}), bf16[128,64,128]{2,1,0:T(8,128)(2,1)S(1)}, u32[]{:S(2)}, u32[]{:S(2)}) async-start(bf16[128,64,128]{2,1,0:T(8,128)(2,1)} %gather_fusion.4), calls=%async_computation.4 | async-start | bytes 4194304 | tf_op jit(solution)/shard_map/all_to_all | solution.py:142
  483.4 7.6 %divide_convert_fusion = bf16[6,640,128]{2,1,0:T(8,128)(2,1)S(1)} fusion(f32[6,640]{1,0:T(8,128)S(1)} %bitcast.152, bf16[6,640,1280]{1,2,0:T(8,128)(2,1)} %get-tuple-element.52, bf16[6,1280,128]{2,1,0:T(8,128)(2,1)} %bitcast.141), kind=kOutput, calls=%fused_computation.25 | convolution fusion | flops 1259274240 | bytes 12794880 | tf_op jit(solution)/shard_map/hqk,hkd->hqd/dot_general | solution.py:136
  493.2 88.5 %all-to-all-done.4 = bf16[128,64,128]{2,1,0:T(8,128)(2,1)S(1)} async-done(((bf16[128,64,128]{2,1,0:T(8,128)(2,1)}), bf16[128,64,128]{2,1,0:T(8,128)(2,1)S(1)}, u32[]{:S(2)}, u32[]{:S(2)}) %all-to-all-start.4) | async-done | bytes 2097184 | tf_op jit(solution)/shard_map/all_to_all | solution.py:142
  581.7 9.1 %all-to-all-start.6 = ((bf16[128,64,128]{2,1,0:T(8,128)(2,1)}), bf16[128,64,128]{2,1,0:T(8,128)(2,1)}, u32[]{:S(2)}, u32[]{:S(2)}) async-start(bf16[128,64,128]{2,1,0:T(8,128)(2,1)} %gather_fusion.6), calls=%async_computation.6 | async-start | bytes 4194304 | tf_op jit(solution)/shard_map/all_to_all | solution.py:142
  597.3 91.5 %all-to-all-done.6 = bf16[128,64,128]{2,1,0:T(8,128)(2,1)} async-done(((bf16[128,64,128]{2,1,0:T(8,128)(2,1)}), bf16[128,64,128]{2,1,0:T(8,128)(2,1)}, u32[]{:S(2)}, u32[]{:S(2)}) %all-to-all-start.6) | async-done | bytes 2097184 | tf_op jit(solution)/shard_map/all_to_all | solution.py:142
  688.8 4.2 all-to-all-start.5
  698.0 8.4 %all-to-all-done.5 = bf16[4,128,768]{2,1,0:T(8,128)(2,1)} async-done(((bf16[4,128,768]{2,1,0:T(8,128)(2,1)}), bf16[4,128,768]{2,1,0:T(8,128)(2,1)}, u32[]{:S(2)}, u32[]{:S(2)}) %all-to-all-start.5) | async-done | bytes 786464 | tf_op jit(solution)/shard_map/all_to_all | solution.py:150
  706.5 3.7 all-to-all-start.7
  712.5 10.5 %all-to-all-done.7 = bf16[4,128,768]{2,1,0:T(8,128)(2,1)S(1)} async-done(((bf16[4,128,768]{2,1,0:T(8,128)(2,1)}), bf16[4,128,768]{2,1,0:T(8,128)(2,1)S(1)}, u32[]{:S(2)}, u32[]{:S(2)}) %all-to-all-start.7) | async-done | bytes 786464 | tf_op jit(solution)/shard_map/all_to_all | solution.py:150
  (180 shorter events, 75.1 us)
Async XLA Ops:
  2.6 15.8 %copy-start.1 = (bf16[256,3072]{1,0:T(8,128)(2,1)S(1)}, bf16[256,3072]{1,0:T(8,128)(2,1)}, u32[]{:S(2)}) copy-start(bf16[256,3072]{1,0:T(8,128)(2,1)} %param.6) | copy-start | bytes 4718596
  2.6 25.3 %all-to-all-start = ((bf16[256,4,768]{0,2,1:T(8,128)(2,1)}), bf16[256,4,768]{0,2,1:T(8,128)(2,1)S(1)}, u32[]{:S(2)}, u32[]{:S(2)}) async-start(bf16[256,4,768]{0,2,1:T(8,128)(2,1)} %bitcast.13), calls=%async_computation | async-start | bytes 3145728 | tf_op jit(solution)/shard_map/all_to_all | solution.py:61
  17.1 2.9 copy-start.2
  17.1 3.1 copy-start.3
  20.0 11.5 %copy-start.4 = (s32[6144]{0:T(1024)S(1)}, s32[6144]{0:T(1024)}, u32[]{:S(2)}) copy-start(s32[6144]{0:T(1024)} %broadcast_in_dim.110) | copy-start | bytes 73732
  27.9 23.4 %all-to-all-start.2 = ((bf16[256,4,768]{0,2,1:T(8,128)(2,1)}), bf16[256,4,768]{0,2,1:T(8,128)(2,1)S(1)}, u32[]{:S(2)}, u32[]{:S(2)}) async-start(bf16[256,4,768]{0,2,1:T(8,128)(2,1)} %bitcast.132), calls=%async_computation.2 | async-start | bytes 3145728 | tf_op jit(solution)/shard_map/all_to_all | solution.py:62
  51.3 207.2 %all-to-all-start.1 = ((bf16[128,128,128]{2,1,0:T(8,128)(2,1)}), bf16[128,128,128]{2,1,0:T(8,128)(2,1)}, u32[]{:S(2)}, u32[]{:S(2)}) async-start(bf16[128,128,128]{2,1,0:T(8,128)(2,1)} %gather_fusion), calls=%async_computation.1 | async-start | bytes 8388608 | tf_op jit(solution)/shard_map/all_to_all | solution.py:106
  258.4 197.1 %all-to-all-start.3 = ((bf16[128,128,128]{2,1,0:T(8,128)(2,1)}), bf16[128,128,128]{2,1,0:T(8,128)(2,1)}, u32[]{:S(2)}, u32[]{:S(2)}) async-start(bf16[128,128,128]{2,1,0:T(8,128)(2,1)} %gather_fusion.2), calls=%async_computation.3 | async-start | bytes 8388608 | tf_op jit(solution)/shard_map/all_to_all | solution.py:109
  464.5 7.8 %copy-start = (bf16[60,128,128]{2,1,0:T(8,128)(2,1)}, bf16[60,128,128]{2,1,0:T(8,128)(2,1)S(1)}, u32[]{:S(2)}) copy-start(bf16[60,128,128]{2,1,0:T(8,128)(2,1)S(1)} %gather_fusion.3) | copy-start | bytes 5898244
  474.5 107.2 %all-to-all-start.4 = ((bf16[128,64,128]{2,1,0:T(8,128)(2,1)}), bf16[128,64,128]{2,1,0:T(8,128)(2,1)S(1)}, u32[]{:S(2)}, u32[]{:S(2)}) async-start(bf16[128,64,128]{2,1,0:T(8,128)(2,1)} %gather_fusion.4), calls=%async_computation.4 | async-start | bytes 4194304 | tf_op jit(solution)/shard_map/all_to_all | solution.py:142
  581.7 107.1 %all-to-all-start.6 = ((bf16[128,64,128]{2,1,0:T(8,128)(2,1)}), bf16[128,64,128]{2,1,0:T(8,128)(2,1)}, u32[]{:S(2)}, u32[]{:S(2)}) async-start(bf16[128,64,128]{2,1,0:T(8,128)(2,1)} %gather_fusion.6), calls=%async_computation.6 | async-start | bytes 4194304 | tf_op jit(solution)/shard_map/all_to_all | solution.py:142
  688.8 17.7 %all-to-all-start.5 = ((bf16[4,128,768]{2,1,0:T(8,128)(2,1)}), bf16[4,128,768]{2,1,0:T(8,128)(2,1)}, u32[]{:S(2)}, u32[]{:S(2)}) async-start(bf16[4,128,768]{2,1,0:T(8,128)(2,1)} %all_to_all.69), calls=%async_computation.5 | async-start | bytes 1572864 | tf_op jit(solution)/shard_map/all_to_all | solution.py:150
  706.5 16.5 %all-to-all-start.7 = ((bf16[4,128,768]{2,1,0:T(8,128)(2,1)}), bf16[4,128,768]{2,1,0:T(8,128)(2,1)S(1)}, u32[]{:S(2)}, u32[]{:S(2)}) async-start(bf16[4,128,768]{2,1,0:T(8,128)(2,1)} %all_to_all.73), calls=%async_computation.7 | async-start | bytes 1572864 | tf_op jit(solution)/shard_map/all_to_all | solution.py:150

commit v2 on v1

--- a/solution.py
+++ b/solution.py
@@ -57,17 +57,16 @@
     group_rows = capacity * BLK
     send_rows = seq_count * slot_count
     score_scale = 1.0 / math.sqrt(head_dim)
-    keys_local, values_local = (
-        lax.all_to_all(query_key, "fsdp", split_axis=1, concat_axis=0, tiled=True),
-        lax.all_to_all(values, "fsdp", split_axis=1, concat_axis=0, tiled=True),
-    )
+    own_blocks = tok_rows // BLK
 
-    def into_items(block_data):
-        shaped = block_data.reshape(shard_blocks, BLK, group_heads, head_dim)
-        return jnp.transpose(shaped, (2, 0, 1, 3)).reshape(item_count, BLK, head_dim)
+    def item_major(block_data):
+        shaped = block_data.reshape(own_blocks, BLK, group_count, group_heads, head_dim)
+        return jnp.transpose(shaped, (2, 3, 0, 1, 4))
 
-    key_items = into_items(keys_local)
-    value_items = into_items(values_local)
+    both = jnp.stack([item_major(query_key), item_major(values)], axis=1)
+    both = lax.all_to_all(both, "fsdp", split_axis=0, concat_axis=3, tiled=True)
+    key_items = both[0, 0].reshape(item_count, BLK, head_dim)
+    value_items = both[0, 1].reshape(item_count, BLK, head_dim)
     group_ids = lax.dynamic_slice_in_dim(cluster_ids, group_index * group_heads, group_heads, 0)
     by_source = jnp.transpose(
         group_ids.reshape(group_heads, seq_count, shard_blocks), (1, 0, 2)
@@ -124,36 +123,28 @@
         one_head,
         (key_grouped.reshape(group_heads, group_rows, head_dim), positions, alive_rows),
     )
-    half = BLK // 2
     value_rows = value_grouped.reshape(group_heads, group_rows, head_dim)
     back_match = source_row[None, :] == row_ids[:, None]
     back_pick = jnp.sum(
         jnp.where(back_match, slot_ids[None, :], 0), axis=1
     ) + group_heads * capacity * (1 - jnp.any(back_match, axis=1).astype(jnp.int32))
-    pieces = []
-    for part in range(2):
-        part_weights = (weights_0, weights_1)[part]
+    halves = []
+    for part_weights, part_total in ((weights_0, totals_0), (weights_1, totals_1)):
         weighted = jnp.einsum(
             "hqk,hkd->hqd", part_weights, value_rows, preferred_element_type=jnp.float32
         )
-        part_total = (totals_0, totals_1)[part]
         outputs = (weighted / part_total).astype(jnp.bfloat16)
-        outputs = outputs.reshape(group_heads * capacity, half, head_dim)
-        returned = lax.all_to_all(
-            by_index(outputs, back_pick), "seq", split_axis=0, concat_axis=0, tiled=True
-        )
-        own_output = by_index(returned, own_pos)
-        token_major = jnp.transpose(
-            own_output.reshape(group_heads, shard_blocks, half, head_dim), (1, 2, 0, 3)
-        ).reshape(shard_blocks * half, group_heads * head_dim)
-        pieces.append(
-            lax.all_to_all(token_major, "fsdp", split_axis=0, concat_axis=1, tiled=True)
-        )
-    own_blocks = tok_rows // BLK
-    joined = jnp.stack(
-        [piece.reshape(own_blocks, half, heads_all * head_dim) for piece in pieces], axis=1
+        halves.append(outputs.reshape(group_heads * capacity, BLK // 2, head_dim))
+    outputs = jnp.concatenate(halves, axis=1)
+    returned = lax.all_to_all(
+        by_index(outputs, back_pick), "seq", split_axis=0, concat_axis=0, tiled=True
     )
-    return joined.reshape(tok_rows, heads_all * head_dim)
+    own_output = by_index(returned, own_pos).reshape(
+        group_heads, group_count, own_blocks, BLK, head_dim
+    )
+    gathered = lax.all_to_all(own_output, "fsdp", split_axis=1, concat_axis=0, tiled=True)
+    token_major = jnp.transpose(gathered[:, 0], (1, 2, 0, 3))
+    return token_major.reshape(tok_rows, heads_all * head_dim)
 
 
 def solution(mesh):

time: 735 us -> 733 us (level)
  the two profiles are of different devices: /device:TPU:32 before, /device:TPU:70 now
where the time goes in v2:
time: 733 us; the launch traced here: 732 us
  waiting for transfers between devices  533 us (73%)
  local copies, waits for them, and re-layouts  77.9 us (11%)
  starting transfers between devices  41.3 us (6%)
  other arithmetic  30.2 us (4%)
  matrix products  24.6 us (3%)
  blocking collectives  23.6 us (3%)
    all_to_all x1, waiting for transfers between devices, shards(): lax.all_to_all(by_index(outputs, back_pick), 'seq', split_axis=0, concat_...  188 us
    all_to_all x1, waiting for transfers between devices, shards(): lax.all_to_all(by_index(key_items, send_pick), 'seq', split_axis=0, conca...  185 us
    all_to_all x1, waiting for transfers between devices, shards(): lax.all_to_all(by_index(value_items, send_pick), 'seq', split_axis=0, con...  137 us
    all_to_all x1, blocking collectives, shards(): lax.all_to_all(own_output, 'fsdp', split_axis=1, concat_axis=0, tiled=True)  23.6 us
    all_to_all x1, waiting for transfers between devices, shards(): both = lax.all_to_all(both, 'fsdp', split_axis=0, concat_axis=3, tiled=True)  22.9 us
    all_to_all x1, starting transfers between devices, shards(): lax.all_to_all(by_index(key_items, send_pick), 'seq', split_axis=0, conca...  18.9 us
    gather x6, local copies, waits for them, and re-layouts, by_index(): return padded[row_index]  18.6 us
    concatenate x5, local copies, waits for them, and re-layouts, by_index(): jnp.concatenate([source_table, jnp.zeros((1,) + source_table.shape[1:], s...  17.7 us
  transfers between devices with their start and end apart: 4, of which 4 were waited for; matrix products, arithmetic and copies ran while one was open for 9% of the time, Pallas kernels for 0%

profile of v2, /device:TPU:70, one launch (start us, length us, event | category | flops | bytes accessed | tf_op | source)
XLA Modules:
  0.0 731.6 jit_solution(10092197036304769592)
XLA Ops:
  5.7 6.1 pad_maximum_fusion
  11.8 4.4 copy.74
  16.2 4.5 all-to-all-start
  35.4 22.9 %all-to-all-done = bf16[4,2,6,2,128,128]{4,3,5,2,1,0:T(2,128)(2,1)S(1)} async-done(((bf16[4,2,6,2,128,128]{4,3,5,2,1,0:T(2,128)(2,1)}), bf16[4,2,6,2,128,128]{4,3,5,2,1,0:T(2,128)(2,1)S(1)}, u32[]{:S(2)}, u32[]{:S(2)}) %all-to-all-start) | async-done | bytes 3145760 | tf_op jit(solution)/shard_map/all_to_all | solution.py:67
  58.2 5.4 copy.75
  63.6 2.2 fusion.22
  66.0 3.1 gather_fusion
  69.1 18.9 %all-to-all-start.1 = ((bf16[128,128,128]{2,1,0:T(8,128)(2,1)}), bf16[128,128,128]{2,1,0:T(8,128)(2,1)}, u32[]{:S(2)}, u32[]{:S(2)}) async-start(bf16[128,128,128]{2,1,0:T(8,128)(2,1)} %gather_fusion), calls=%async_computation.1 | async-start | bytes 8388608 | tf_op jit(solution)/shard_map/all_to_all | solution.py:105
  88.4 3.2 gather_fusion.2
  91.5 184.7 %all-to-all-done.1 = bf16[128,128,128]{2,1,0:T(8,128)(2,1)} async-done(((bf16[128,128,128]{2,1,0:T(8,128)(2,1)}), bf16[128,128,128]{2,1,0:T(8,128)(2,1)}, u32[]{:S(2)}, u32[]{:S(2)}) %all-to-all-start.1) | async-done | bytes 4194336 | tf_op jit(solution)/shard_map/all_to_all | solution.py:105
  276.2 8.9 %all-to-all-start.2 = ((bf16[128,128,128]{2,1,0:T(8,128)(2,1)}), bf16[128,128,128]{2,1,0:T(8,128)(2,1)}, u32[]{:S(2)}, u32[]{:S(2)}) async-start(bf16[128,128,128]{2,1,0:T(8,128)(2,1)} %gather_fusion.2), calls=%async_computation.2 | async-start | bytes 8388608 | tf_op jit(solution)/shard_map/all_to_all | solution.py:108
  285.6 5.8 concatenate.22
  291.5 3.1 gather_fusion.1
  294.6 41.4 %while.16 = (s32[]{:T(128)}, bf16[6,640,1280]{1,2,0:T(8,128)(2,1)}, bf16[6,640,1280]{1,2,0:T(8,128)(2,1)}, f32[6,640,1]{1,0,2:T(8,128)S(1)}, f32[6,640,1]{1,0,2:...) while((s32[]{:T(128)}, bf16[6,640,1280]{1,2,0:T(8,128)(2,1)}, ...), condition=%wide.region_12.13_spmd, body=%wide.region_9.12_spmd.sunk | while | flops 437451520 | bytes 25025912 | solution.py:122
  296.7 2.4 fusion.34
  303.5 2.4 fusion.34
  310.4 2.4 fusion.34
  317.2 2.4 fusion.34
  324.1 2.4 fusion.34
  330.9 2.4 fusion.34
  333.4 2.0 fusion.35
  336.0 137.3 %all-to-all-done.2 = bf16[128,128,128]{2,1,0:T(8,128)(2,1)} async-done(((bf16[128,128,128]{2,1,0:T(8,128)(2,1)}), bf16[128,128,128]{2,1,0:T(8,128)(2,1)}, u32[]{:S(2)}, u32[]{:S(2)}) %all-to-all-start.2) | async-done | bytes 4194336 | tf_op jit(solution)/shard_map/all_to_all | solution.py:108
  473.3 5.8 concatenate.24
  479.1 3.1 gather_fusion.3
  482.2 7.0 divide_convert_fusion.1
  489.3 7.0 divide_convert_fusion
  496.5 3.0 gather_fusion.4
  499.5 8.9 %all-to-all-start.3 = ((bf16[128,128,128]{2,1,0:T(8,128)(2,1)}), bf16[128,128,128]{2,1,0:T(8,128)(2,1)}, u32[]{:S(2)}, u32[]{:S(2)}) async-start(bf16[128,128,128]{2,1,0:T(8,128)(2,1)} %gather_fusion.4), calls=%async_computation.3 | async-start | bytes 8388608 | tf_op jit(solution)/shard_map/all_to_all | solution.py:139
  508.5 188.1 %all-to-all-done.3 = bf16[128,128,128]{2,1,0:T(8,128)(2,1)} async-done(((bf16[128,128,128]{2,1,0:T(8,128)(2,1)}), bf16[128,128,128]{2,1,0:T(8,128)(2,1)}, u32[]{:S(2)}, u32[]{:S(2)}) %all-to-all-start.3) | async-done | bytes 4194336 | tf_op jit(solution)/shard_map/all_to_all | solution.py:139
  696.6 5.7 concatenate.27
  702.3 3.0 gather_fusion.5
  705.5 23.6 %all_to_all.48 = bf16[6,4,2,128,128]{4,3,2,0,1:T(8,128)(2,1)S(1)} all-to-all(bf16[6,4,2,128,128]{4,3,2,0,1:T(8,128)(2,1)S(1)} %copy.81), channel_id=1, replica_groups=mesh['seq'=128,'fsdp'=4] {'fsdp'}, dimensions={1} | all-to-all | bytes 3145728 | tf_op jit(solution)/shard_map/all_to_all | solution.py:145
  (152 shorter events, 48.2 us)
Async XLA Ops:
  16.2 42.0 %all-to-all-start = ((bf16[4,2,6,2,128,128]{4,3,5,2,1,0:T(2,128)(2,1)}), bf16[4,2,6,2,128,128]{4,3,5,2,1,0:T(2,128)(2,1)S(1)}, u32[]{:S(2)}, u32[]{:S(2)}) async-start(bf16[4,2,6,2,128,128]{4,3,5,2,1,0:T(2,128)(2,1)} %copy.74), calls=%async_computation | async-start | bytes 6291456 | tf_op jit(solution)/shard_map/all_to_all | solution.py:67
  69.1 207.1 %all-to-all-start.1 = ((bf16[128,128,128]{2,1,0:T(8,128)(2,1)}), bf16[128,128,128]{2,1,0:T(8,128)(2,1)}, u32[]{:S(2)}, u32[]{:S(2)}) async-start(bf16[128,128,128]{2,1,0:T(8,128)(2,1)} %gather_fusion), calls=%async_computation.1 | async-start | bytes 8388608 | tf_op jit(solution)/shard_map/all_to_all | solution.py:105
  276.2 197.1 %all-to-all-start.2 = ((bf16[128,128,128]{2,1,0:T(8,128)(2,1)}), bf16[128,128,128]{2,1,0:T(8,128)(2,1)}, u32[]{:S(2)}, u32[]{:S(2)}) async-start(bf16[128,128,128]{2,1,0:T(8,128)(2,1)} %gather_fusion.2), calls=%async_computation.2 | async-start | bytes 8388608 | tf_op jit(solution)/shard_map/all_to_all | solution.py:108
  499.5 197.1 %all-to-all-start.3 = ((bf16[128,128,128]{2,1,0:T(8,128)(2,1)}), bf16[128,128,128]{2,1,0:T(8,128)(2,1)}, u32[]{:S(2)}, u32[]{:S(2)}) async-start(bf16[128,128,128]{2,1,0:T(8,128)(2,1)} %gather_fusion.4), calls=%async_computation.3 | async-start | bytes 8388608 | tf_op jit(solution)/shard_map/all_to_all | solution.py:139

commit v3 on v2

--- a/solution.py
+++ b/solution.py
@@ -12,10 +12,7 @@
 
 
 def by_index(source_table, row_index):
-    padded = jnp.concatenate(
-        [source_table, jnp.zeros((1,) + source_table.shape[1:], source_table.dtype)], axis=0
-    )
-    return padded[row_index]
+    return source_table[jnp.clip(row_index, 0, source_table.shape[0] - 1)]
 
 
 def softmax_group(key_rows, positions, alive_rows, score_scale):
@@ -59,14 +56,17 @@
     score_scale = 1.0 / math.sqrt(head_dim)
     own_blocks = tok_rows // BLK
 
-    def item_major(block_data):
-        shaped = block_data.reshape(own_blocks, BLK, group_count, group_heads, head_dim)
-        return jnp.transpose(shaped, (2, 3, 0, 1, 4))
+    keys_local, values_local = (
+        lax.all_to_all(query_key, "fsdp", split_axis=1, concat_axis=0, tiled=True),
+        lax.all_to_all(values, "fsdp", split_axis=1, concat_axis=0, tiled=True),
+    )
 
-    both = jnp.stack([item_major(query_key), item_major(values)], axis=1)
-    both = lax.all_to_all(both, "fsdp", split_axis=0, concat_axis=3, tiled=True)
-    key_items = both[0, 0].reshape(item_count, BLK, head_dim)
-    value_items = both[0, 1].reshape(item_count, BLK, head_dim)
+    def into_items(block_data):
+        shaped = block_data.reshape(shard_blocks, BLK, group_heads, head_dim)
+        return jnp.transpose(shaped, (2, 0, 1, 3)).reshape(item_count, BLK, head_dim)
+
+    key_items = into_items(keys_local)
+    value_items = into_items(values_local)
     group_ids = lax.dynamic_slice_in_dim(cluster_ids, group_index * group_heads, group_heads, 0)
     by_source = jnp.transpose(
         group_ids.reshape(group_heads, seq_count, shard_blocks), (1, 0, 2)

time: 733 us -> 703 us (0.959)
  local copies, waits for them, and re-layouts: 77.9 us -> 57.9 us
  other arithmetic: 30.2 us -> 22.1 us
    concatenate x5 -> x0, local copies, waits for them, and re-layouts: 17.7 us -> none  [by_index(): jnp.concatenate([source_table, jnp.zeros((1,) + source_table.shape[1:], s...]
    all_to_all x1 -> x2, waiting for transfers between devices: 22.9 us -> 14.9 us  [the longest x1 7.55 us: shards(): lax.all_to_all(values, 'fsdp', split_axis=1, concat_axis=0, tiled=True)]
  transfers between devices with their start and end apart: 4 -> 5, of which waited for: 4 -> 5; matrix products, arithmetic and copies ran while one was open for 9% -> 11% of each run, Pallas kernels for 0% -> 0%
where the time goes in v3:
time: 703 us; the launch traced here: 702 us
  waiting for transfers between devices  528 us (75%)
  local copies, waits for them, and re-layouts  57.9 us (8%)
  starting transfers between devices  45.1 us (6%)
  matrix products  24.7 us (4%)
  blocking collectives  23.6 us (3%)
  other arithmetic  22.1 us (3%)
    all_to_all x1, waiting for transfers between devices, shards(): lax.all_to_all(by_index(outputs, back_pick), 'seq', split_axis=0, concat_...  188 us
    all_to_all x1, waiting for transfers between devices, shards(): lax.all_to_all(by_index(key_items, send_pick), 'seq', split_axis=0, conca...  182 us
    all_to_all x1, waiting for transfers between devices, shards(): lax.all_to_all(by_index(value_items, send_pick), 'seq', split_axis=0, con...  143 us
    all_to_all x1, blocking collectives, shards(): lax.all_to_all(own_output, 'fsdp', split_axis=1, concat_axis=0, tiled=True)  23.6 us
    all_to_all x1, starting transfers between devices, shards(): lax.all_to_all(by_index(key_items, send_pick), 'seq', split_axis=0, conca...  18.9 us
    gather x6, local copies, waits for them, and re-layouts, by_index(): return source_table[jnp.clip(row_index, 0, source_table.shape[0] - 1)]  18.6 us
    reduce_sum x6, other arithmetic, softmax_group(): jnp.sum(weights, axis=1, keepdims=True)  14.4 us
  transfers between devices with their start and end apart: 5, of which 5 were waited for; matrix products, arithmetic and copies ran while one was open for 11% of the time, Pallas kernels for 0%

profile of v3, /device:TPU:70, one launch (start us, length us, event | category | flops | bytes accessed | tf_op | source)
XLA Modules:
  0.0 702.3 jit_solution(313478013310527961)
XLA Ops:
  0.0 2.6 copy.78
  2.6 4.5 all-to-all-start
  20.4 7.3 %all-to-all-done = bf16[256,4,768]{0,2,1:T(8,128)(2,1)S(1)} async-done(((bf16[256,4,768]{0,2,1:T(8,128)(2,1)}), bf16[256,4,768]{0,2,1:T(8,128)(2,1)S(1)}, u32[]{:S(2)}, u32[]{:S(2)}) %all-to-all-start) | async-done | bytes 1572896 | tf_op jit(solution)/shard_map/all_to_all | solution.py:60
  27.7 3.6 all-to-all-start.2
  32.3 2.4 copy.79
  34.7 3.6 reshape.278
  38.3 2.1 copy.80
  40.5 3.1 gather_fusion
  43.6 7.5 %all-to-all-done.2 = bf16[256,4,768]{0,2,1:T(8,128)(2,1)S(1)} async-done(((bf16[256,4,768]{0,2,1:T(8,128)(2,1)}), bf16[256,4,768]{0,2,1:T(8,128)(2,1)S(1)}, u32[]{:S(2)}, u32[]{:S(2)}) %all-to-all-start.2) | async-done | bytes 1572896 | tf_op jit(solution)/shard_map/all_to_all | solution.py:61
  51.1 18.9 %all-to-all-start.1 = ((bf16[128,128,128]{2,1,0:T(8,128)(2,1)}), bf16[128,128,128]{2,1,0:T(8,128)(2,1)}, u32[]{:S(2)}, u32[]{:S(2)}) async-start(bf16[128,128,128]{2,1,0:T(8,128)(2,1)} %gather_fusion), calls=%async_computation.1 | async-start | bytes 8388608 | tf_op jit(solution)/shard_map/all_to_all | solution.py:105
  73.2 3.1 gather_fusion.2
  76.3 181.9 %all-to-all-done.1 = bf16[128,128,128]{2,1,0:T(8,128)(2,1)} async-done(((bf16[128,128,128]{2,1,0:T(8,128)(2,1)}), bf16[128,128,128]{2,1,0:T(8,128)(2,1)}, u32[]{:S(2)}, u32[]{:S(2)}) %all-to-all-start.1) | async-done | bytes 4194336 | tf_op jit(solution)/shard_map/all_to_all | solution.py:105
  258.2 9.0 %all-to-all-start.3 = ((bf16[128,128,128]{2,1,0:T(8,128)(2,1)}), bf16[128,128,128]{2,1,0:T(8,128)(2,1)}, u32[]{:S(2)}, u32[]{:S(2)}) async-start(bf16[128,128,128]{2,1,0:T(8,128)(2,1)} %gather_fusion.2), calls=%async_computation.3 | async-start | bytes 8388608 | tf_op jit(solution)/shard_map/all_to_all | solution.py:108
  267.7 3.1 gather_fusion.1
  270.8 41.2 %while.16 = (s32[]{:T(128)}, bf16[6,640,1280]{1,2,0:T(8,128)(2,1)}, bf16[6,640,1280]{1,2,0:T(8,128)(2,1)}, f32[6,640,1]{1,0,2:T(8,128)S(1)}, f32[6,640,1]{1,0,2:...) while((s32[]{:T(128)}, bf16[6,640,1280]{1,2,0:T(8,128)(2,1)}, ...), condition=%wide.region_12.13_spmd, body=%wide.region_9.12_spmd.sunk | while | flops 437451520 | bytes 25025912 | solution.py:122
  272.9 2.4 fusion.31
  279.7 2.4 fusion.31
  286.6 2.4 fusion.31
  293.4 2.4 fusion.31
  295.8 2.0 fusion.32
  300.3 2.4 fusion.31
  307.1 2.4 fusion.31
  309.6 2.0 fusion.32
  312.0 143.3 %all-to-all-done.3 = bf16[128,128,128]{2,1,0:T(8,128)(2,1)} async-done(((bf16[128,128,128]{2,1,0:T(8,128)(2,1)}), bf16[128,128,128]{2,1,0:T(8,128)(2,1)}, u32[]{:S(2)}, u32[]{:S(2)}) %all-to-all-start.3) | async-done | bytes 4194336 | tf_op jit(solution)/shard_map/all_to_all | solution.py:108
  455.3 3.1 gather_fusion.3
  458.4 7.0 %divide_convert_fusion.1 = bf16[6,640,128]{2,1,0:T(8,128)(2,1)S(1)} fusion(f32[6,640]{1,0:T(8,128)S(1)} %bitcast.157, bf16[6,640,1280]{1,2,0:T(8,128)(2,1)} %get-tuple-element.50, bf16[6,1280,128]{2,1,0:T(8,128)(2,1)S(1)} %bitcast.146), kind=kOutput, calls=%fused_computation.25 | convolution fusion | flops 1259274240 | bytes 12794880 | tf_op jit(solution)/shard_map/hqk,hkd->hqd/dot_general | solution.py:133
  465.4 7.0 %divide_convert_fusion = bf16[6,640,128]{2,1,0:T(8,128)(2,1)S(1)} fusion(f32[6,640]{1,0:T(8,128)S(1)} %bitcast.158, bf16[6,640,1280]{1,2,0:T(8,128)(2,1)} %get-tuple-element.52, bf16[6,1280,128]{2,1,0:T(8,128)(2,1)S(1)} %bitcast.147), kind=kOutput, calls=%fused_computation.24 | convolution fusion | flops 1259274240 | bytes 12794880 | tf_op jit(solution)/shard_map/hqk,hkd->hqd/dot_general | solution.py:133
  472.6 3.1 gather_fusion.4
  475.7 9.2 %all-to-all-start.4 = ((bf16[128,128,128]{2,1,0:T(8,128)(2,1)}), bf16[128,128,128]{2,1,0:T(8,128)(2,1)}, u32[]{:S(2)}, u32[]{:S(2)}) async-start(bf16[128,128,128]{2,1,0:T(8,128)(2,1)} %gather_fusion.4), calls=%async_computation.4 | async-start | bytes 8388608 | tf_op jit(solution)/shard_map/all_to_all | solution.py:139
  484.9 188.1 %all-to-all-done.4 = bf16[128,128,128]{2,1,0:T(8,128)(2,1)} async-done(((bf16[128,128,128]{2,1,0:T(8,128)(2,1)}), bf16[128,128,128]{2,1,0:T(8,128)(2,1)}, u32[]{:S(2)}, u32[]{:S(2)}) %all-to-all-start.4) | async-done | bytes 4194336 | tf_op jit(solution)/shard_map/all_to_all | solution.py:139
  673.0 3.0 gather_fusion.5
  676.2 23.6 %all_to_all.62 = bf16[6,4,2,128,128]{4,3,2,0,1:T(8,128)(2,1)S(1)} all-to-all(bf16[6,4,2,128,128]{4,3,2,0,1:T(8,128)(2,1)S(1)} %copy.89), channel_id=1, replica_groups=mesh['seq'=128,'fsdp'=4] {'fsdp'}, dimensions={1} | all-to-all | bytes 3145728 | tf_op jit(solution)/shard_map/all_to_all | solution.py:145
  (157 shorter events, 42.8 us)
Async XLA Ops:
  2.6 25.2 %all-to-all-start = ((bf16[256,4,768]{0,2,1:T(8,128)(2,1)}), bf16[256,4,768]{0,2,1:T(8,128)(2,1)S(1)}, u32[]{:S(2)}, u32[]{:S(2)}) async-start(bf16[256,4,768]{0,2,1:T(8,128)(2,1)} %bitcast.13), calls=%async_computation | async-start | bytes 3145728 | tf_op jit(solution)/shard_map/all_to_all | solution.py:60
  7.0 11.3 %copy-start = (bf16[256,3072]{1,0:T(8,128)(2,1)S(1)}, bf16[256,3072]{1,0:T(8,128)(2,1)}, u32[]{:S(2)}) copy-start(bf16[256,3072]{1,0:T(8,128)(2,1)} %param.6) | copy-start | bytes 4718596
  17.1 2.9 copy-start.1
  17.1 3.1 copy-start.2
  19.9 11.4 %copy-start.3 = (s32[6144]{0:T(1024)S(1)}, s32[6144]{0:T(1024)}, u32[]{:S(2)}) copy-start(s32[6144]{0:T(1024)} %broadcast_in_dim.108) | copy-start | bytes 73732
  27.7 23.4 %all-to-all-start.2 = ((bf16[256,4,768]{0,2,1:T(8,128)(2,1)}), bf16[256,4,768]{0,2,1:T(8,128)(2,1)S(1)}, u32[]{:S(2)}, u32[]{:S(2)}) async-start(bf16[256,4,768]{0,2,1:T(8,128)(2,1)} %bitcast.140), calls=%async_computation.2 | async-start | bytes 3145728 | tf_op jit(solution)/shard_map/all_to_all | solution.py:61
  51.1 207.1 %all-to-all-start.1 = ((bf16[128,128,128]{2,1,0:T(8,128)(2,1)}), bf16[128,128,128]{2,1,0:T(8,128)(2,1)}, u32[]{:S(2)}, u32[]{:S(2)}) async-start(bf16[128,128,128]{2,1,0:T(8,128)(2,1)} %gather_fusion), calls=%async_computation.1 | async-start | bytes 8388608 | tf_op jit(solution)/shard_map/all_to_all | solution.py:105
  258.2 197.1 %all-to-all-start.3 = ((bf16[128,128,128]{2,1,0:T(8,128)(2,1)}), bf16[128,128,128]{2,1,0:T(8,128)(2,1)}, u32[]{:S(2)}, u32[]{:S(2)}) async-start(bf16[128,128,128]{2,1,0:T(8,128)(2,1)} %gather_fusion.2), calls=%async_computation.3 | async-start | bytes 8388608 | tf_op jit(solution)/shard_map/all_to_all | solution.py:108
  475.7 197.3 %all-to-all-start.4 = ((bf16[128,128,128]{2,1,0:T(8,128)(2,1)}), bf16[128,128,128]{2,1,0:T(8,128)(2,1)}, u32[]{:S(2)}, u32[]{:S(2)}) async-start(bf16[128,128,128]{2,1,0:T(8,128)(2,1)} %gather_fusion.4), calls=%async_computation.4 | async-start | bytes 8388608 | tf_op jit(solution)/shard_map/all_to_all | solution.py:139

commit v4 on v3

--- a/solution.py
+++ b/solution.py
@@ -56,9 +56,24 @@
     score_scale = 1.0 / math.sqrt(head_dim)
     own_blocks = tok_rows // BLK
 
-    keys_local, values_local = (
-        lax.all_to_all(query_key, "fsdp", split_axis=1, concat_axis=0, tiled=True),
-        lax.all_to_all(values, "fsdp", split_axis=1, concat_axis=0, tiled=True),
+    keys_local = lax.all_to_all(query_key, "fsdp", split_axis=1, concat_axis=0, tiled=True)
+    value_chunks = values.reshape(tok_rows, group_count, group_heads * head_dim)
+    value_chunks, keys_local = lax.optimization_barrier((value_chunks, keys_local))
+    by_shift = [lax.dynamic_index_in_dim(value_chunks, group_index, 1, keepdims=False)]
+    for shift in range(1, group_count):
+        outgoing = lax.dynamic_index_in_dim(
+            value_chunks, (group_index + shift) % group_count, 1, keepdims=False
+        )
+        by_shift.append(
+            lax.ppermute(
+                outgoing,
+                "fsdp",
+                [(peer, (peer + shift) % group_count) for peer in range(group_count)],
+            )
+        )
+    source_order = (group_index - jnp.arange(group_count, dtype=jnp.int32)) % group_count
+    values_local = jnp.stack(by_shift)[source_order].reshape(
+        group_count * tok_rows, group_heads * head_dim
     )
 
     def into_items(block_data):
@@ -105,9 +120,9 @@
     arrived_k = lax.all_to_all(
         by_index(key_items, send_pick), "seq", split_axis=0, concat_axis=0, tiled=True
     )
-    arrived_v = lax.all_to_all(
-        by_index(value_items, send_pick), "seq", split_axis=0, concat_axis=0, tiled=True
-    )
+    value_send = by_index(value_items, send_pick)
+    arrived_k, value_send = lax.optimization_barrier((arrived_k, value_send))
+    arrived_v = lax.all_to_all(value_send, "seq", split_axis=0, concat_axis=0, tiled=True)
     key_grouped = by_index(arrived_k, source_row)
     value_grouped = by_index(arrived_v, source_row)
     positions = (block_of[:, None] * BLK + jnp.arange(BLK, dtype=jnp.int32)[None, :]).reshape(
@@ -142,8 +157,10 @@
     own_output = by_index(returned, own_pos).reshape(
         group_heads, group_count, own_blocks, BLK, head_dim
     )
-    gathered = lax.all_to_all(own_output, "fsdp", split_axis=1, concat_axis=0, tiled=True)
-    token_major = jnp.transpose(gathered[:, 0], (1, 2, 0, 3))
+    gathered = lax.all_to_all(
+        jnp.swapaxes(own_output, 0, 1), "fsdp", split_axis=0, concat_axis=0, tiled=True
+    )
+    token_major = jnp.transpose(gathered, (2, 3, 0, 1, 4))
     return token_major.reshape(tok_rows, heads_all * head_dim)
 
 

time: 703 us -> 688 us (0.979)
  waiting for transfers between devices: 528 us -> 499 us
    all_to_all x1, waiting for transfers between devices: 182 us -> 155 us  [shards(): lax.all_to_all(by_index(key_items, send_pick), 'seq', split_axis=0, conca...]
    ppermute x0 -> x3, waiting for transfers between devices: none -> 15.8 us  [shards(): lax.ppermute(outgoing, 'fsdp', [(peer, (peer + shift) % group_count) for...]
    all_to_all x2 -> x1, waiting for transfers between devices: 151 us -> 136 us  [shards(): lax.all_to_all(value_send, 'seq', split_axis=0, concat_axis=0, tiled=True)]
    ppermute x0 -> x3, starting transfers between devices: none -> 8.97 us  [shards(): lax.ppermute(outgoing, 'fsdp', [(peer, (peer + shift) % group_count) for...]
  transfers between devices with their start and end apart: 5 -> 7, of which waited for: 5 -> 6; matrix products, arithmetic and copies ran while one was open for 11% -> 11% of each run, Pallas kernels for 0% -> 0%
where the time goes in v4:
time: 688 us; the launch traced here: 687 us
  waiting for transfers between devices  499 us (73%)
  local copies, waits for them, and re-layouts  63.1 us (9%)
  starting transfers between devices  50.8 us (7%)
  matrix products  24.6 us (4%)
  other arithmetic  24.1 us (4%)
  blocking collectives  23.6 us (3%)
    all_to_all x1, waiting for transfers between devices, shards(): lax.all_to_all(by_index(outputs, back_pick), 'seq', split_axis=0, concat_...  188 us
    all_to_all x1, waiting for transfers between devices, shards(): lax.all_to_all(by_index(key_items, send_pick), 'seq', split_axis=0, conca...  155 us
    all_to_all x1, waiting for transfers between devices, shards(): lax.all_to_all(value_send, 'seq', split_axis=0, concat_axis=0, tiled=True)  136 us
    all_to_all x1, blocking collectives, shards(): lax.all_to_all(jnp.swapaxes(own_output, 0, 1), 'fsdp', split_axis=0, conc...  23.6 us
    gather x6, local copies, waits for them, and re-layouts, by_index(): return source_table[jnp.clip(row_index, 0, source_table.shape[0] - 1)]  19.8 us
    all_to_all x1, starting transfers between devices, shards(): lax.all_to_all(by_index(key_items, send_pick), 'seq', split_axis=0, conca...  19.1 us
    ppermute x3, waiting for transfers between devices, shards(): lax.ppermute(outgoing, 'fsdp', [(peer, (peer + shift) % group_count) for...  15.8 us
    reduce_sum x6, other arithmetic, softmax_group(): jnp.sum(weights, axis=1, keepdims=True)  14.5 us
  transfers between devices with their start and end apart: 7, of which 6 were waited for; matrix products, arithmetic and copies ran while one was open for 11% of the time, Pallas kernels for 0%

profile of v4, /device:TPU:70, one launch (start us, length us, event | category | flops | bytes accessed | tf_op | source)
XLA Modules:
  0.0 686.5 jit_solution(17942411138984894427)
XLA Ops:
  0.0 2.6 copy.99
  2.6 4.5 all-to-all-start
  23.9 3.9 all-to-all-done
  30.8 3.1 gather_fusion
  33.9 19.1 %all-to-all-start.1 = ((bf16[128,128,128]{2,1,0:T(8,128)(2,1)}), bf16[128,128,128]{2,1,0:T(8,128)(2,1)}, u32[]{:S(2)}, u32[]{:S(2)}) async-start(bf16[128,128,128]{2,1,0:T(8,128)(2,1)} %gather_fusion), calls=%async_computation.1 | async-start | bytes 8388608 | tf_op jit(solution)/shard_map/all_to_all | solution.py:120
  53.7 2.5 collective-permute-start
  56.2 4.0 collective-permute-start.1
  60.2 2.5 collective-permute-start.2
  63.1 13.2 %collective-permute-done = bf16[256,768]{1,0:T(8,128)(2,1)S(1)} collective-permute-done((bf16[256,768]{1,0:T(8,128)(2,1)S(1)}, bf16[256,768]{1,0:T(8,128)(2,1)S(1)}, u32[]{:S(2)}, u32[]{:S(2)}) %collective-permute-start) | collective-permute-done | bytes 393248 | tf_op jit(solution)/shard_map/ppermute | solution.py:68
  76.4 2.5 collective-permute-done.2
  82.6 3.1 gather_fusion.2
  85.7 155.4 %all-to-all-done.1 = bf16[128,128,128]{2,1,0:T(8,128)(2,1)} async-done(((bf16[128,128,128]{2,1,0:T(8,128)(2,1)}), bf16[128,128,128]{2,1,0:T(8,128)(2,1)}, u32[]{:S(2)}, u32[]{:S(2)}) %all-to-all-start.1) | async-done | bytes 4194336 | tf_op jit(solution)/shard_map/all_to_all | solution.py:120
  241.1 9.0 %all-to-all-start.2 = ((bf16[128,128,128]{2,1,0:T(8,128)(2,1)}), bf16[128,128,128]{2,1,0:T(8,128)(2,1)}, u32[]{:S(2)}, u32[]{:S(2)}) async-start(bf16[128,128,128]{2,1,0:T(8,128)(2,1)} %gather_fusion.2), calls=%async_computation.2 | async-start | bytes 8388608 | tf_op jit(solution)/shard_map/all_to_all | solution.py:125
  250.5 4.3 gather_fusion.3
  254.8 47.0 %while.16 = (s32[]{:T(128)}, bf16[6,640,1280]{1,2,0:T(8,128)(2,1)}, bf16[6,640,1280]{1,2,0:T(8,128)(2,1)}, f32[6,640,1]{1,0,2:T(8,128)S(1)}, f32[6,640,1]{1,0,2:...) while((s32[]{:T(128)}, bf16[6,640,1280]{1,2,0:T(8,128)(2,1)}, ...), condition=%wide.region_12.13_spmd, body=%wide.region_9.12_spmd.sunk | while | flops 437451520 | bytes 25025412 | solution.py:137
  258.0 2.4 fusion.33
  265.9 2.4 fusion.33
  273.7 2.4 fusion.33
  281.5 2.4 fusion.33
  289.3 2.4 fusion.33
  297.2 2.4 fusion.33
  299.8 2.0 fusion.34
  301.8 136.4 %all-to-all-done.2 = bf16[128,128,128]{2,1,0:T(8,128)(2,1)} async-done(((bf16[128,128,128]{2,1,0:T(8,128)(2,1)}), bf16[128,128,128]{2,1,0:T(8,128)(2,1)}, u32[]{:S(2)}, u32[]{:S(2)}) %all-to-all-start.2) | async-done | bytes 4194336 | tf_op jit(solution)/shard_map/all_to_all | solution.py:125
  438.2 3.1 gather_fusion.4
  441.3 7.0 %divide_convert_fusion = bf16[6,640,128]{2,1,0:T(8,128)(2,1)S(1)} fusion(f32[6,640]{1,0:T(8,128)S(1)} %bitcast.167, bf16[6,640,1280]{1,2,0:T(8,128)(2,1)} %get-tuple-element.60, bf16[6,1280,128]{2,1,0:T(8,128)(2,1)S(1)} %bitcast.149), kind=kOutput, calls=%fused_computation.25 | convolution fusion | flops 1259274240 | bytes 12794880 | tf_op jit(solution)/shard_map/hqk,hkd->hqd/dot_general | solution.py:148
  448.4 7.0 %divide_convert_fusion.1 = bf16[6,640,128]{2,1,0:T(8,128)(2,1)S(1)} fusion(f32[6,640]{1,0:T(8,128)S(1)} %bitcast.168, bf16[6,640,1280]{1,2,0:T(8,128)(2,1)} %get-tuple-element.57, bf16[6,1280,128]{2,1,0:T(8,128)(2,1)S(1)} %bitcast.150), kind=kOutput, calls=%fused_computation.26 | convolution fusion | flops 1259274240 | bytes 12794880 | tf_op jit(solution)/shard_map/hqk,hkd->hqd/dot_general | solution.py:148
  455.6 3.1 gather_fusion.5
  458.6 9.3 %all-to-all-start.3 = ((bf16[128,128,128]{2,1,0:T(8,128)(2,1)}), bf16[128,128,128]{2,1,0:T(8,128)(2,1)}, u32[]{:S(2)}, u32[]{:S(2)}) async-start(bf16[128,128,128]{2,1,0:T(8,128)(2,1)} %gather_fusion.5), calls=%async_computation.3 | async-start | bytes 8388608 | tf_op jit(solution)/shard_map/all_to_all | solution.py:154
  468.0 188.1 %all-to-all-done.3 = bf16[128,128,128]{2,1,0:T(8,128)(2,1)} async-done(((bf16[128,128,128]{2,1,0:T(8,128)(2,1)}), bf16[128,128,128]{2,1,0:T(8,128)(2,1)}, u32[]{:S(2)}, u32[]{:S(2)}) %all-to-all-start.3) | async-done | bytes 4194336 | tf_op jit(solution)/shard_map/all_to_all | solution.py:154
  656.0 3.0 gather_fusion.6
  659.3 23.6 %all_to_all.39 = bf16[4,6,2,128,128]{4,3,2,1,0:T(8,128)(2,1)S(1)} all-to-all(bf16[4,6,2,128,128]{4,3,2,1,0:T(8,128)(2,1)S(1)} %copy.114), channel_id=1, replica_groups=mesh['seq'=128,'fsdp'=4] {'fsdp'}, dimensions={0} | all-to-all | bytes 3145728 | tf_op jit(solution)/shard_map/all_to_all | solution.py:160
  683.9 2.6 reshape.399
  (189 shorter events, 56.3 us)
Async XLA Ops:
  2.6 25.2 %all-to-all-start = ((bf16[256,4,768]{0,2,1:T(8,128)(2,1)}), bf16[256,4,768]{0,2,1:T(8,128)(2,1)S(1)}, u32[]{:S(2)}, u32[]{:S(2)}) async-start(bf16[256,4,768]{0,2,1:T(8,128)(2,1)} %bitcast.14), calls=%async_computation | async-start | bytes 3145728 | tf_op jit(solution)/shard_map/all_to_all | solution.py:59
  7.0 13.1 %copy-start.1 = (bf16[256,3072]{1,0:T(8,128)(2,1)S(1)}, bf16[256,3072]{1,0:T(8,128)(2,1)}, u32[]{:S(2)}) copy-start(bf16[256,3072]{1,0:T(8,128)(2,1)} %param.6) | copy-start | bytes 4718596
  15.4 0.5 copy-start.7
  15.9 1.2 copy-start.9
  20.1 1.7 copy-start.2
  20.1 2.0 copy-start.3
  20.1 2.0 copy-start.4
  33.9 19.1 %copy-start = (bf16[256,3072]{0,1:T(8,128)(2,1)S(1)}, bf16[256,3072]{0,1:T(8,128)(2,1)}, u32[]{:S(2)}) copy-start(bf16[256,3072]{0,1:T(8,128)(2,1)} %copy.98) | copy-start | bytes 4718596
  33.9 207.2 %all-to-all-start.1 = ((bf16[128,128,128]{2,1,0:T(8,128)(2,1)}), bf16[128,128,128]{2,1,0:T(8,128)(2,1)}, u32[]{:S(2)}, u32[]{:S(2)}) async-start(bf16[128,128,128]{2,1,0:T(8,128)(2,1)} %gather_fusion), calls=%async_computation.1 | async-start | bytes 8388608 | tf_op jit(solution)/shard_map/all_to_all | solution.py:120
  53.7 22.7 %collective-permute-start = (bf16[256,768]{1,0:T(8,128)(2,1)S(1)}, bf16[256,768]{1,0:T(8,128)(2,1)S(1)}, u32[]{:S(2)}, u32[]{:S(2)}) collective-permute-start(bf16[256,768]{1,0:T(8,128)(2,1)S(1)} %bitcast.163), channel_id=1, source_target_pairs={{0,1},{1,2},{2,3},{3,0},{4,5},{5,6},{6,7},{7,4},{8,9},{9,10},{10,1... | collective-permute-start | bytes 1179656 | tf_op jit(solution)/shard_map/ppermute | solution.py:68
  56.2 20.2 %collective-permute-start.1 = (bf16[256,768]{1,0:T(8,128)(2,1)S(1)}, bf16[256,768]{1,0:T(8,128)(2,1)S(1)}, u32[]{:S(2)}, u32[]{:S(2)}) collective-permute-start(bf16[256,768]{1,0:T(8,128)(2,1)S(1)} %bitcast.162), channel_id=1, source_target_pairs={{0,2},{1,3},{2,0},{3,1},{4,6},{5,7},{6,4},{7,5},{8,10},{9,11},{10,... | collective-permute-start | bytes 1179656 | tf_op jit(solution)/shard_map/ppermute | solution.py:68
  60.2 18.7 %collective-permute-start.2 = (bf16[256,768]{1,0:T(8,128)(2,1)S(1)}, bf16[256,768]{1,0:T(8,128)(2,1)S(1)}, u32[]{:S(2)}, u32[]{:S(2)}) collective-permute-start(bf16[256,768]{1,0:T(8,128)(2,1)S(1)} %bitcast.161), channel_id=1, source_target_pairs={{0,3},{1,0},{2,1},{3,2},{4,7},{5,4},{6,5},{7,6},{8,11},{9,8},{10,9... | collective-permute-start | bytes 1179656 | tf_op jit(solution)/shard_map/ppermute | solution.py:68
  85.7 164.4 %copy-start.6 = (s32[60]{0:T(128)S(1)}, s32[60]{0:T(128)}, u32[]{:S(2)}) copy-start(s32[60]{0:T(128)} %get-tuple-element.63) | copy-start | bytes 724
  85.7 164.6 %copy-start.5 = (s32[128]{0:T(128)S(1)}, s32[128]{0:T(128)}, u32[]{:S(2)}) copy-start(s32[128]{0:T(128)} %get-tuple-element.98) | copy-start | bytes 1540
  241.1 197.1 %all-to-all-start.2 = ((bf16[128,128,128]{2,1,0:T(8,128)(2,1)}), bf16[128,128,128]{2,1,0:T(8,128)(2,1)}, u32[]{:S(2)}, u32[]{:S(2)}) async-start(bf16[128,128,128]{2,1,0:T(8,128)(2,1)} %gather_fusion.2), calls=%async_computation.2 | async-start | bytes 8388608 | tf_op jit(solution)/shard_map/all_to_all | solution.py:125
  250.5 4.3 copy-start.11
  250.5 4.3 copy-start.12
  458.6 9.3 %copy-start.8 = (s32[48]{0:T(128)S(1)}, s32[48]{0:T(128)}, u32[]{:S(2)}) copy-start(s32[48]{0:T(128)} %copy-done.7) | copy-start | bytes 580
  458.6 9.3 %copy-start.10 = (s32[48]{0:T(128)S(1)}, s32[48]{0:T(128)}, u32[]{:S(2)}) copy-start(s32[48]{0:T(128)} %copy-done.9) | copy-start | bytes 580
  458.6 197.4 %all-to-all-start.3 = ((bf16[128,128,128]{2,1,0:T(8,128)(2,1)}), bf16[128,128,128]{2,1,0:T(8,128)(2,1)}, u32[]{:S(2)}, u32[]{:S(2)}) async-start(bf16[128,128,128]{2,1,0:T(8,128)(2,1)} %gather_fusion.5), calls=%async_computation.3 | async-start | bytes 8388608 | tf_op jit(solution)/shard_map/all_to_all | solution.py:154

commit v5 on v4

--- a/solution.py
+++ b/solution.py
@@ -13,6 +13,23 @@
 
 def by_index(source_table, row_index):
     return source_table[jnp.clip(row_index, 0, source_table.shape[0] - 1)]
+
+
+def fsdp_exchange(outgoing_by_dest, group_index, group_count):
+    by_shift = [lax.dynamic_index_in_dim(outgoing_by_dest, group_index, 0, keepdims=False)]
+    for shift in range(1, group_count):
+        outgoing = lax.dynamic_index_in_dim(
+            outgoing_by_dest, (group_index + shift) % group_count, 0, keepdims=False
+        )
+        by_shift.append(
+            lax.ppermute(
+                outgoing,
+                "fsdp",
+                [(peer, (peer + shift) % group_count) for peer in range(group_count)],
+            )
+        )
+    source_order = (group_index - jnp.arange(group_count, dtype=jnp.int32)) % group_count
+    return jnp.stack(by_shift)[source_order]
 
 
 def softmax_group(key_rows, positions, alive_rows, score_scale):
@@ -157,9 +174,7 @@
     own_output = by_index(returned, own_pos).reshape(
         group_heads, group_count, own_blocks, BLK, head_dim
     )
-    gathered = lax.all_to_all(
-        jnp.swapaxes(own_output, 0, 1), "fsdp", split_axis=0, concat_axis=0, tiled=True
-    )
+    gathered = fsdp_exchange(jnp.swapaxes(own_output, 0, 1), group_index, group_count)
     token_major = jnp.transpose(gathered, (2, 3, 0, 1, 4))
     return token_major.reshape(tok_rows, heads_all * head_dim)
 

time: 688 us -> 691 us (level)
  blocking collectives: 23.6 us -> 0 us
  waiting for transfers between devices: 499 us -> 513 us
  starting transfers between devices: 50.8 us -> 60.3 us
    all_to_all x1 -> x0, blocking collectives: 23.6 us -> none  [shards(): lax.all_to_all(jnp.swapaxes(own_output, 0, 1), 'fsdp', split_axis=0, conc...]
    ppermute x0 -> x3, waiting for transfers between devices: none -> 13.3 us  [fsdp_exchange(): lax.ppermute(outgoing, 'fsdp', [(peer, (peer + shift) % group_count) for...]
    ppermute x0 -> x3, starting transfers between devices: none -> 9.52 us  [fsdp_exchange(): lax.ppermute(outgoing, 'fsdp', [(peer, (peer + shift) % group_count) for...]
  transfers between devices with their start and end apart: 7 -> 10, of which waited for: 6 -> 8; matrix products, arithmetic and copies ran while one was open for 11% -> 11% of each run, Pallas kernels for 0% -> 0%
where the time goes in v5:
time: 691 us; the launch traced here: 689 us
  waiting for transfers between devices  513 us (74%)
  local copies, waits for them, and re-layouts  66.4 us (10%)
  starting transfers between devices  60.3 us (9%)
  matrix products  24.6 us (4%)
  other arithmetic  24.3 us (4%)
    all_to_all x1, waiting for transfers between devices, shards(): lax.all_to_all(by_index(outputs, back_pick), 'seq', split_axis=0, concat_...  188 us
    all_to_all x1, waiting for transfers between devices, shards(): lax.all_to_all(by_index(key_items, send_pick), 'seq', split_axis=0, conca...  155 us
    all_to_all x1, waiting for transfers between devices, shards(): lax.all_to_all(value_send, 'seq', split_axis=0, concat_axis=0, tiled=True)  136 us
    gather x6, local copies, waits for them, and re-layouts, by_index(): return source_table[jnp.clip(row_index, 0, source_table.shape[0] - 1)]  19.8 us
    all_to_all x1, starting transfers between devices, shards(): lax.all_to_all(by_index(key_items, send_pick), 'seq', split_axis=0, conca...  19.1 us
    ppermute x3, waiting for transfers between devices, shards(): lax.ppermute(outgoing, 'fsdp', [(peer, (peer + shift) % group_count) for...  15.8 us
    reduce_sum x6, other arithmetic, softmax_group(): jnp.sum(weights, axis=1, keepdims=True)  14.5 us
    dot_general x2, matrix products, shards(): jnp.einsum('hqk,hkd->hqd', part_weights, value_rows, preferred_element_ty...  14 us
  transfers between devices with their start and end apart: 10, of which 8 were waited for; matrix products, arithmetic and copies ran while one was open for 11% of the time, Pallas kernels for 0%

profile of v5, /device:TPU:70, one launch (start us, length us, event | category | flops | bytes accessed | tf_op | source)
XLA Modules:
  0.0 689.2 jit_solution(16110161066629940773)
XLA Ops:
  0.0 2.6 copy.86
  2.6 4.5 all-to-all-start
  23.9 3.9 all-to-all-done
  30.8 3.1 gather_fusion
  33.9 19.1 %all-to-all-start.1 = ((bf16[128,128,128]{2,1,0:T(8,128)(2,1)}), bf16[128,128,128]{2,1,0:T(8,128)(2,1)}, u32[]{:S(2)}, u32[]{:S(2)}) async-start(bf16[128,128,128]{2,1,0:T(8,128)(2,1)} %gather_fusion), calls=%async_computation.1 | async-start | bytes 8388608 | tf_op jit(solution)/shard_map/all_to_all | solution.py:137
  53.7 2.5 collective-permute-start
  56.2 4.0 collective-permute-start.1
  60.2 2.5 collective-permute-start.2
  63.1 13.2 %collective-permute-done = bf16[256,768]{1,0:T(8,128)(2,1)S(1)} collective-permute-done((bf16[256,768]{1,0:T(8,128)(2,1)S(1)}, bf16[256,768]{1,0:T(8,128)(2,1)S(1)}, u32[]{:S(2)}, u32[]{:S(2)}) %collective-permute-start) | collective-permute-done | bytes 393248 | tf_op jit(solution)/shard_map/ppermute | solution.py:85
  76.4 2.5 collective-permute-done.2
  82.6 3.1 gather_fusion.2
  85.7 155.4 %all-to-all-done.1 = bf16[128,128,128]{2,1,0:T(8,128)(2,1)} async-done(((bf16[128,128,128]{2,1,0:T(8,128)(2,1)}), bf16[128,128,128]{2,1,0:T(8,128)(2,1)}, u32[]{:S(2)}, u32[]{:S(2)}) %all-to-all-start.1) | async-done | bytes 4194336 | tf_op jit(solution)/shard_map/all_to_all | solution.py:137
  241.1 9.0 %all-to-all-start.2 = ((bf16[128,128,128]{2,1,0:T(8,128)(2,1)}), bf16[128,128,128]{2,1,0:T(8,128)(2,1)}, u32[]{:S(2)}, u32[]{:S(2)}) async-start(bf16[128,128,128]{2,1,0:T(8,128)(2,1)} %gather_fusion.2), calls=%async_computation.2 | async-start | bytes 8388608 | tf_op jit(solution)/shard_map/all_to_all | solution.py:142
  250.5 4.3 gather_fusion.3
  254.8 47.0 %while.16 = (s32[]{:T(128)}, bf16[6,640,1280]{1,2,0:T(8,128)(2,1)}, bf16[6,640,1280]{1,2,0:T(8,128)(2,1)}, f32[6,640,1]{1,0,2:T(8,128)S(1)}, f32[6,640,1]{1,0,2:...) while((s32[]{:T(128)}, bf16[6,640,1280]{1,2,0:T(8,128)(2,1)}, ...), condition=%wide.region_12.13_spmd, body=%wide.region_9.12_spmd.sunk | while | flops 437451520 | bytes 25025412 | solution.py:154
  258.0 2.4 fusion.33
  265.9 2.4 fusion.33
  301.8 136.4 %all-to-all-done.2 = bf16[128,128,128]{2,1,0:T(8,128)(2,1)} async-done(((bf16[128,128,128]{2,1,0:T(8,128)(2,1)}), bf16[128,128,128]{2,1,0:T(8,128)(2,1)}, u32[]{:S(2)}, u32[]{:S(2)}) %all-to-all-start.2) | async-done | bytes 4194336 | tf_op jit(solution)/shard_map/all_to_all | solution.py:142
  438.2 3.1 gather_fusion.4
  441.3 7.0 %divide_convert_fusion = bf16[6,640,128]{2,1,0:T(8,128)(2,1)S(1)} fusion(f32[6,640]{1,0:T(8,128)S(1)} %bitcast.187, bf16[6,640,1280]{1,2,0:T(8,128)(2,1)} %get-tuple-element.60, bf16[6,1280,128]{2,1,0:T(8,128)(2,1)S(1)} %bitcast.166), kind=kOutput, calls=%fused_computation.26 | convolution fusion | flops 1259274240 | bytes 12794880 | tf_op jit(solution)/shard_map/hqk,hkd->hqd/dot_general | solution.py:165
  448.4 7.0 %divide_convert_fusion.1 = bf16[6,640,128]{2,1,0:T(8,128)(2,1)S(1)} fusion(f32[6,640]{1,0:T(8,128)S(1)} %bitcast.188, bf16[6,640,1280]{1,2,0:T(8,128)(2,1)} %get-tuple-element.57, bf16[6,1280,128]{2,1,0:T(8,128)(2,1)S(1)} %bitcast.167), kind=kOutput, calls=%fused_computation.27 | convolution fusion | flops 1259274240 | bytes 12794880 | tf_op jit(solution)/shard_map/hqk,hkd->hqd/dot_general | solution.py:165
  455.6 3.1 gather_fusion.5
  458.6 9.3 %all-to-all-start.3 = ((bf16[128,128,128]{2,1,0:T(8,128)(2,1)}), bf16[128,128,128]{2,1,0:T(8,128)(2,1)}, u32[]{:S(2)}, u32[]{:S(2)}) async-start(bf16[128,128,128]{2,1,0:T(8,128)(2,1)} %gather_fusion.5), calls=%async_computation.3 | async-start | bytes 8388608 | tf_op jit(solution)/shard_map/all_to_all | solution.py:171
  468.0 188.1 %all-to-all-done.3 = bf16[128,128,128]{2,1,0:T(8,128)(2,1)} async-done(((bf16[128,128,128]{2,1,0:T(8,128)(2,1)}), bf16[128,128,128]{2,1,0:T(8,128)(2,1)}, u32[]{:S(2)}, u32[]{:S(2)}) %all-to-all-start.3) | async-done | bytes 4194336 | tf_op jit(solution)/shard_map/all_to_all | solution.py:171
  656.0 3.0 gather_fusion.6
  659.2 2.5 collective-permute-start.4
  661.7 3.4 collective-permute-start.3
  665.1 3.7 collective-permute-start.5
  668.8 5.9 collective-permute-done.4
  674.7 7.4 %collective-permute-done.3 = bf16[6,2,128,128]{3,2,1,0:T(8,128)(2,1)S(1)} collective-permute-done((bf16[6,2,128,128]{3,2,1,0:T(8,128)(2,1)S(1)}, bf16[6,2,128,128]{3,2,1,0:T(8,128)(2,1)S(1)}, u32[]{:S(2)}, u32[]{:S(2)}) %collective-permute-start.3) | collective-permute-done | bytes 393248 | tf_op jit(solution)/shard_map/ppermute | solution.py:25
  684.1 2.5 copy.109
  686.6 2.6 reshape.414
  (196 shorter events, 69.0 us)
Async XLA Ops:
  2.6 25.2 %all-to-all-start = ((bf16[256,4,768]{0,2,1:T(8,128)(2,1)}), bf16[256,4,768]{0,2,1:T(8,128)(2,1)S(1)}, u32[]{:S(2)}, u32[]{:S(2)}) async-start(bf16[256,4,768]{0,2,1:T(8,128)(2,1)} %bitcast.14), calls=%async_computation | async-start | bytes 3145728 | tf_op jit(solution)/shard_map/all_to_all | solution.py:76
  7.0 13.1 %copy-start.1 = (bf16[256,3072]{1,0:T(8,128)(2,1)S(1)}, bf16[256,3072]{1,0:T(8,128)(2,1)}, u32[]{:S(2)}) copy-start(bf16[256,3072]{1,0:T(8,128)(2,1)} %param.6) | copy-start | bytes 4718596
  15.4 0.5 copy-start.7
  15.9 1.2 copy-start.9
  20.1 1.7 copy-start.2
  20.1 2.0 copy-start.3
  20.1 2.0 copy-start.4
  33.9 19.1 %copy-start = (bf16[256,3072]{0,1:T(8,128)(2,1)S(1)}, bf16[256,3072]{0,1:T(8,128)(2,1)}, u32[]{:S(2)}) copy-start(bf16[256,3072]{0,1:T(8,128)(2,1)} %copy.85) | copy-start | bytes 4718596
  33.9 207.2 %all-to-all-start.1 = ((bf16[128,128,128]{2,1,0:T(8,128)(2,1)}), bf16[128,128,128]{2,1,0:T(8,128)(2,1)}, u32[]{:S(2)}, u32[]{:S(2)}) async-start(bf16[128,128,128]{2,1,0:T(8,128)(2,1)} %gather_fusion), calls=%async_computation.1 | async-start | bytes 8388608 | tf_op jit(solution)/shard_map/all_to_all | solution.py:137
  53.7 22.7 %collective-permute-start = (bf16[256,768]{1,0:T(8,128)(2,1)S(1)}, bf16[256,768]{1,0:T(8,128)(2,1)S(1)}, u32[]{:S(2)}, u32[]{:S(2)}) collective-permute-start(bf16[256,768]{1,0:T(8,128)(2,1)S(1)} %bitcast.183), channel_id=1, source_target_pairs={{0,1},{1,2},{2,3},{3,0},{4,5},{5,6},{6,7},{7,4},{8,9},{9,10},{10,1... | collective-permute-start | bytes 1179656 | tf_op jit(solution)/shard_map/ppermute | solution.py:85
  56.2 20.2 %collective-permute-start.1 = (bf16[256,768]{1,0:T(8,128)(2,1)S(1)}, bf16[256,768]{1,0:T(8,128)(2,1)S(1)}, u32[]{:S(2)}, u32[]{:S(2)}) collective-permute-start(bf16[256,768]{1,0:T(8,128)(2,1)S(1)} %bitcast.182), channel_id=1, source_target_pairs={{0,2},{1,3},{2,0},{3,1},{4,6},{5,7},{6,4},{7,5},{8,10},{9,11},{10,... | collective-permute-start | bytes 1179656 | tf_op jit(solution)/shard_map/ppermute | solution.py:85
  60.2 18.7 %collective-permute-start.2 = (bf16[256,768]{1,0:T(8,128)(2,1)S(1)}, bf16[256,768]{1,0:T(8,128)(2,1)S(1)}, u32[]{:S(2)}, u32[]{:S(2)}) collective-permute-start(bf16[256,768]{1,0:T(8,128)(2,1)S(1)} %bitcast.181), channel_id=1, source_target_pairs={{0,3},{1,0},{2,1},{3,2},{4,7},{5,4},{6,5},{7,6},{8,11},{9,8},{10,9... | collective-permute-start | bytes 1179656 | tf_op jit(solution)/shard_map/ppermute | solution.py:85
  85.7 164.4 %copy-start.6 = (s32[60]{0:T(128)S(1)}, s32[60]{0:T(128)}, u32[]{:S(2)}) copy-start(s32[60]{0:T(128)} %get-tuple-element.63) | copy-start | bytes 724
  85.7 164.6 %copy-start.5 = (s32[128]{0:T(128)S(1)}, s32[128]{0:T(128)}, u32[]{:S(2)}) copy-start(s32[128]{0:T(128)} %get-tuple-element.102) | copy-start | bytes 1540
  241.1 197.1 %all-to-all-start.2 = ((bf16[128,128,128]{2,1,0:T(8,128)(2,1)}), bf16[128,128,128]{2,1,0:T(8,128)(2,1)}, u32[]{:S(2)}, u32[]{:S(2)}) async-start(bf16[128,128,128]{2,1,0:T(8,128)(2,1)} %gather_fusion.2), calls=%async_computation.2 | async-start | bytes 8388608 | tf_op jit(solution)/shard_map/all_to_all | solution.py:142
  250.5 4.3 copy-start.11
  250.5 4.3 copy-start.12
  458.6 9.3 %copy-start.8 = (s32[48]{0:T(128)S(1)}, s32[48]{0:T(128)}, u32[]{:S(2)}) copy-start(s32[48]{0:T(128)} %copy-done.7) | copy-start | bytes 580
  458.6 9.3 %copy-start.10 = (s32[48]{0:T(128)S(1)}, s32[48]{0:T(128)}, u32[]{:S(2)}) copy-start(s32[48]{0:T(128)} %copy-done.9) | copy-start | bytes 580
  458.6 197.4 %all-to-all-start.3 = ((bf16[128,128,128]{2,1,0:T(8,128)(2,1)}), bf16[128,128,128]{2,1,0:T(8,128)(2,1)}, u32[]{:S(2)}, u32[]{:S(2)}) async-start(bf16[128,128,128]{2,1,0:T(8,128)(2,1)} %gather_fusion.5), calls=%async_computation.3 | async-start | bytes 8388608 | tf_op jit(solution)/shard_map/all_to_all | solution.py:171
  659.2 15.4 %collective-permute-start.4 = (bf16[6,2,128,128]{3,2,1,0:T(8,128)(2,1)S(1)}, bf16[6,2,128,128]{3,2,1,0:T(8,128)(2,1)S(1)}, u32[]{:S(2)}, u32[]{:S(2)}) collective-permute-start(bf16[6,2,128,128]{3,2,1,0:T(8,128)(2,1)S(1)} %get-tuple-element.94), channel_id=1, source_target_pairs={{0,2},{1,3},{2,0},{3,1},{4,6},{5,7},{6,4},{7,5},{8,10},{9,11},{10,... | collective-permute-start | bytes 1179656 | tf_op jit(solution)/shard_map/ppermute | solution.py:25
  661.7 20.3 %collective-permute-start.3 = (bf16[6,2,128,128]{3,2,1,0:T(8,128)(2,1)S(1)}, bf16[6,2,128,128]{3,2,1,0:T(8,128)(2,1)S(1)}, u32[]{:S(2)}, u32[]{:S(2)}) collective-permute-start(bf16[6,2,128,128]{3,2,1,0:T(8,128)(2,1)S(1)} %get-tuple-element.95), channel_id=1, source_target_pairs={{0,1},{1,2},{2,3},{3,0},{4,5},{5,6},{6,7},{7,4},{8,9},{9,10},{10,1... | collective-permute-start | bytes 1179656 | tf_op jit(solution)/shard_map/ppermute | solution.py:25
  665.1 16.9 %collective-permute-start.5 = (bf16[6,2,128,128]{3,2,1,0:T(8,128)(2,1)S(1)}, bf16[6,2,128,128]{3,2,1,0:T(8,128)(2,1)S(1)}, u32[]{:S(2)}, u32[]{:S(2)}) collective-permute-start(bf16[6,2,128,128]{3,2,1,0:T(8,128)(2,1)S(1)} %get-tuple-element.96), channel_id=1, source_target_pairs={{0,3},{1,0},{2,1},{3,2},{4,7},{5,4},{6,5},{7,6},{8,11},{9,8},{10,9... | collective-permute-start | bytes 1179656 | tf_op jit(solution)/shard_map/ppermute | solution.py:25

commit v6 on v4

--- a/solution.py
+++ b/solution.py
@@ -16,25 +16,13 @@
 
 
 def softmax_group(key_rows, positions, alive_rows, score_scale):
-    half = BLK // 2
-    blocks = key_rows.shape[0] // BLK
-
-    def by_half(rows):
-        shaped = rows.reshape((blocks, 2, half) + rows.shape[1:])
-        return jnp.swapaxes(shaped, 0, 1).reshape(rows.shape)
-
-    query_rows = by_half(key_rows)
-    query_positions = by_half(positions)
-    query_alive = by_half(alive_rows)
-    scores = jnp.dot(query_rows, key_rows.T, preferred_element_type=jnp.float32) * score_scale
-    allowed = alive_rows[None, :] & (positions[None, :] <= query_positions[:, None])
+    scores = jnp.dot(key_rows, key_rows.T, preferred_element_type=jnp.float32) * score_scale
+    allowed = alive_rows[None, :] & (positions[None, :] <= positions[:, None])
     scores = jnp.where(allowed, scores, masked_score)
     row_peak = jnp.max(scores, axis=1, keepdims=True)
     weights = jnp.where(allowed, jnp.exp(scores - row_peak), 0.0)
-    row_total = jnp.where(query_alive[:, None], jnp.sum(weights, axis=1, keepdims=True), 1.0)
-    weights = weights.astype(jnp.bfloat16).reshape(2, blocks * half, key_rows.shape[0])
-    row_total = row_total.reshape(2, blocks * half, 1)
-    return weights[0], weights[1], row_total[0], row_total[1]
+    row_total = jnp.where(alive_rows[:, None], jnp.sum(weights, axis=1, keepdims=True), 1.0)
+    return weights.astype(jnp.bfloat16), row_total
 
 
 def shards(query_key, values, cluster_ids):
@@ -134,7 +122,7 @@
         key_rows, where_at, alive_here = operands
         return softmax_group(key_rows, where_at, alive_here, score_scale)
 
-    weights_0, weights_1, totals_0, totals_1 = lax.map(
+    weights, totals = lax.map(
         one_head,
         (key_grouped.reshape(group_heads, group_rows, head_dim), positions, alive_rows),
     )
@@ -143,14 +131,8 @@
     back_pick = jnp.sum(
         jnp.where(back_match, slot_ids[None, :], 0), axis=1
     ) + group_heads * capacity * (1 - jnp.any(back_match, axis=1).astype(jnp.int32))
-    halves = []
-    for part_weights, part_total in ((weights_0, totals_0), (weights_1, totals_1)):
-        weighted = jnp.einsum(
-            "hqk,hkd->hqd", part_weights, value_rows, preferred_element_type=jnp.float32
-        )
-        outputs = (weighted / part_total).astype(jnp.bfloat16)
-        halves.append(outputs.reshape(group_heads * capacity, BLK // 2, head_dim))
-    outputs = jnp.concatenate(halves, axis=1)
+    weighted = jnp.einsum("hqk,hkd->hqd", weights, value_rows, preferred_element_type=jnp.float32)
+    outputs = (weighted / totals).astype(jnp.bfloat16).reshape(group_heads * capacity, BLK, head_dim)
     returned = lax.all_to_all(
         by_index(outputs, back_pick), "seq", split_axis=0, concat_axis=0, tiled=True
     )

time: 688 us -> 685 us (level)
  other arithmetic: 24.1 us -> 55.7 us
  waiting for transfers between devices: 499 us -> 481 us
  local copies, waits for them, and re-layouts: 63.1 us -> 51.1 us
    dynamic_update_slice x0 -> x12, other arithmetic: none -> 31.3 us  [shards(): lax.map(one_head, (key_grouped.reshape(group_heads, group_rows, head_dim)...]
    all_to_all x1, waiting for transfers between devices: 136 us -> 121 us  [shards(): lax.all_to_all(value_send, 'seq', split_axis=0, concat_axis=0, tiled=True)]
    dynamic_update_slice x24 -> x6, local copies, waits for them, and re-layouts: 12.9 us -> 0.8 us  [shards(): lax.map(one_head, (key_grouped.reshape(group_heads, group_rows, head_dim)...]
    dot_general x8 -> x7, matrix products: 24.6 us -> 21.3 us  [the longest x1 10.8 us: shards(): jnp.einsum('hqk,hkd->hqd', weights, value_rows, preferred_element_type=jn...]
  transfers between devices with their start and end apart: 7 -> 7, of which waited for: 6 -> 6; matrix products, arithmetic and copies ran while one was open for 11% -> 13% of each run, Pallas kernels for 0% -> 0%
where the time goes in v6:
time: 685 us; the launch traced here: 684 us
  waiting for transfers between devices  481 us (70%)
  other arithmetic  55.7 us (8%)
  local copies, waits for them, and re-layouts  51.1 us (7%)
  starting transfers between devices  50.5 us (7%)
  blocking collectives  23.6 us (3%)
  matrix products  21.3 us (3%)
    all_to_all x1, waiting for transfers between devices, shards(): lax.all_to_all(by_index(outputs, back_pick), 'seq', split_axis=0, concat_...  188 us
    all_to_all x1, waiting for transfers between devices, shards(): lax.all_to_all(by_index(key_items, send_pick), 'seq', split_axis=0, conca...  154 us
    all_to_all x1, waiting for transfers between devices, shards(): lax.all_to_all(value_send, 'seq', split_axis=0, concat_axis=0, tiled=True)  121 us
    dynamic_update_slice x12, other arithmetic, shards(): lax.map(one_head, (key_grouped.reshape(group_heads, group_rows, head_dim)...  31.3 us
    all_to_all x1, blocking collectives, shards(): lax.all_to_all(jnp.swapaxes(own_output, 0, 1), 'fsdp', split_axis=0, conc...  23.6 us
    gather x6, local copies, waits for them, and re-layouts, by_index(): return source_table[jnp.clip(row_index, 0, source_table.shape[0] - 1)]  19.8 us
    all_to_all x1, starting transfers between devices, shards(): lax.all_to_all(by_index(key_items, send_pick), 'seq', split_axis=0, conca...  19.1 us
    ppermute x3, waiting for transfers between devices, shards(): lax.ppermute(outgoing, 'fsdp', [(peer, (peer + shift) % group_count) for...  15.3 us
  transfers between devices with their start and end apart: 7, of which 6 were waited for; matrix products, arithmetic and copies ran while one was open for 13% of the time, Pallas kernels for 0%

profile of v6, /device:TPU:70, one launch (start us, length us, event | category | flops | bytes accessed | tf_op | source)
XLA Modules:
  0.0 684.0 jit_solution(7700841947505605212)
XLA Ops:
  0.0 2.6 copy.81
  2.6 4.5 all-to-all-start
  24.1 3.7 all-to-all-done
  30.8 3.0 gather_fusion
  33.8 19.1 %all-to-all-start.1 = ((bf16[128,128,128]{2,1,0:T(8,128)(2,1)}), bf16[128,128,128]{2,1,0:T(8,128)(2,1)}, u32[]{:S(2)}, u32[]{:S(2)}) async-start(bf16[128,128,128]{2,1,0:T(8,128)(2,1)} %gather_fusion), calls=%async_computation.1 | async-start | bytes 8388608 | tf_op jit(solution)/shard_map/all_to_all | solution.py:108
  55.2 2.5 collective-permute-start
  57.6 4.0 collective-permute-start.1
  61.6 2.5 collective-permute-start.2
  65.0 12.8 %collective-permute-done = bf16[256,768]{1,0:T(8,128)(2,1)S(1)} collective-permute-done((bf16[256,768]{1,0:T(8,128)(2,1)S(1)}, bf16[256,768]{1,0:T(8,128)(2,1)S(1)}, u32[]{:S(2)}, u32[]{:S(2)}) %collective-permute-start) | collective-permute-done | bytes 393248 | tf_op jit(solution)/shard_map/ppermute | solution.py:56
  77.8 2.5 collective-permute-done.2
  84.2 3.3 gather_fusion.2
  87.5 153.6 %all-to-all-done.1 = bf16[128,128,128]{2,1,0:T(8,128)(2,1)} async-done(((bf16[128,128,128]{2,1,0:T(8,128)(2,1)}), bf16[128,128,128]{2,1,0:T(8,128)(2,1)}, u32[]{:S(2)}, u32[]{:S(2)}) %all-to-all-start.1) | async-done | bytes 4194336 | tf_op jit(solution)/shard_map/all_to_all | solution.py:108
  241.0 8.9 %all-to-all-start.2 = ((bf16[128,128,128]{2,1,0:T(8,128)(2,1)}), bf16[128,128,128]{2,1,0:T(8,128)(2,1)}, u32[]{:S(2)}, u32[]{:S(2)}) async-start(bf16[128,128,128]{2,1,0:T(8,128)(2,1)} %gather_fusion.2), calls=%async_computation.2 | async-start | bytes 8388608 | tf_op jit(solution)/shard_map/all_to_all | solution.py:113
  250.1 3.1 gather_fusion.3
  253.2 64.3 %while.12 = (s32[]{:T(128)}, bf16[6,1280,1280]{1,2,0:T(8,128)(2,1)}, f32[6,1280,1]{1,0,2:T(8,128)S(1)}, pred[6,1280]{1,0:T(8,128)(4,1)S(1)}, s32[6,1280]{1,0:T(8...) while((s32[]{:T(128)}, bf16[6,1280,1280]{1,2,0:T(8,128)(2,1)}, ...), condition=%wide.region_12.13_spmd, body=%wide.region_9.12_spmd.sunk | while | flops 444005120 | bytes 49581200 | solution.py:125
  255.9 2.3 fusion.33
  258.8 5.2 fusion.32
  266.6 2.3 fusion.33
  269.5 5.2 fusion.32
  280.2 5.3 fusion.32
  291.0 5.2 fusion.32
  301.7 5.2 fusion.32
  312.4 5.2 fusion.32
  317.6 120.5 %all-to-all-done.2 = bf16[128,128,128]{2,1,0:T(8,128)(2,1)} async-done(((bf16[128,128,128]{2,1,0:T(8,128)(2,1)}), bf16[128,128,128]{2,1,0:T(8,128)(2,1)}, u32[]{:S(2)}, u32[]{:S(2)}) %all-to-all-start.2) | async-done | bytes 4194336 | tf_op jit(solution)/shard_map/all_to_all | solution.py:113
  438.1 4.3 gather_fusion.4
  442.4 10.8 %divide_convert_fusion = bf16[6,1280,128]{2,1,0:T(8,128)(2,1)S(1)} fusion(bf16[6,1280,1280]{1,2,0:T(8,128)(2,1)} %get-tuple-element.45, bf16[6,1280,128]{2,1,0:T(8,128)(2,1)} %bitcast.124, f32[6,1280]{1,0:T(8,128)S(1)} %bitcast.137), kind=kOutput, calls=%fused_computation.22 | convolution fusion | flops 2518548480 | bytes 23623680 | tf_op jit(solution)/shard_map/hqk,hkd->hqd/dot_general | solution.py:134
  453.2 3.1 gather_fusion.5
  456.3 9.1 %all-to-all-start.3 = ((bf16[128,128,128]{2,1,0:T(8,128)(2,1)}), bf16[128,128,128]{2,1,0:T(8,128)(2,1)}, u32[]{:S(2)}, u32[]{:S(2)}) async-start(bf16[128,128,128]{2,1,0:T(8,128)(2,1)} %gather_fusion.5), calls=%async_computation.3 | async-start | bytes 8388608 | tf_op jit(solution)/shard_map/all_to_all | solution.py:136
  465.4 188.1 %all-to-all-done.3 = bf16[128,128,128]{2,1,0:T(8,128)(2,1)} async-done(((bf16[128,128,128]{2,1,0:T(8,128)(2,1)}), bf16[128,128,128]{2,1,0:T(8,128)(2,1)}, u32[]{:S(2)}, u32[]{:S(2)}) %all-to-all-start.3) | async-done | bytes 4194336 | tf_op jit(solution)/shard_map/all_to_all | solution.py:136
  653.5 3.0 gather_fusion.6
  656.7 23.6 %all_to_all.39 = bf16[4,6,2,128,128]{4,3,2,1,0:T(8,128)(2,1)S(1)} all-to-all(bf16[4,6,2,128,128]{4,3,2,1,0:T(8,128)(2,1)S(1)} %copy.95), channel_id=1, replica_groups=mesh['seq'=128,'fsdp'=4] {'fsdp'}, dimensions={0} | all-to-all | bytes 3145728 | tf_op jit(solution)/shard_map/all_to_all | solution.py:142
  681.3 2.6 reshape.374
  (137 shorter events, 56.4 us)
Async XLA Ops:
  2.6 25.2 %all-to-all-start = ((bf16[256,4,768]{0,2,1:T(8,128)(2,1)}), bf16[256,4,768]{0,2,1:T(8,128)(2,1)S(1)}, u32[]{:S(2)}, u32[]{:S(2)}) async-start(bf16[256,4,768]{0,2,1:T(8,128)(2,1)} %bitcast.7), calls=%async_computation | async-start | bytes 3145728 | tf_op jit(solution)/shard_map/all_to_all | solution.py:47
  7.0 13.1 %copy-start.2 = (bf16[256,3072]{1,0:T(8,128)(2,1)S(1)}, bf16[256,3072]{1,0:T(8,128)(2,1)}, u32[]{:S(2)}) copy-start(bf16[256,3072]{1,0:T(8,128)(2,1)} %param.6) | copy-start | bytes 4718596
  15.4 0.5 copy-start.10
  15.9 1.2 copy-start.12
  20.1 1.7 copy-start.3
  20.1 2.0 copy-start.4
  20.1 2.0 copy-start.5
  24.1 6.7 copy-start.7
  33.8 20.7 %copy-start.1 = (bf16[256,3072]{0,1:T(8,128)(2,1)S(1)}, bf16[256,3072]{0,1:T(8,128)(2,1)}, u32[]{:S(2)}) copy-start(bf16[256,3072]{0,1:T(8,128)(2,1)} %copy.80) | copy-start | bytes 4718596
  33.8 207.2 %all-to-all-start.1 = ((bf16[128,128,128]{2,1,0:T(8,128)(2,1)}), bf16[128,128,128]{2,1,0:T(8,128)(2,1)}, u32[]{:S(2)}, u32[]{:S(2)}) async-start(bf16[128,128,128]{2,1,0:T(8,128)(2,1)} %gather_fusion), calls=%async_computation.1 | async-start | bytes 8388608 | tf_op jit(solution)/shard_map/all_to_all | solution.py:108
  55.2 22.7 %collective-permute-start = (bf16[256,768]{1,0:T(8,128)(2,1)S(1)}, bf16[256,768]{1,0:T(8,128)(2,1)S(1)}, u32[]{:S(2)}, u32[]{:S(2)}) collective-permute-start(bf16[256,768]{1,0:T(8,128)(2,1)S(1)} %bitcast.133), channel_id=1, source_target_pairs={{0,1},{1,2},{2,3},{3,0},{4,5},{5,6},{6,7},{7,4},{8,9},{9,10},{10,1... | collective-permute-start | bytes 1179656 | tf_op jit(solution)/shard_map/ppermute | solution.py:56
  57.6 20.2 %collective-permute-start.1 = (bf16[256,768]{1,0:T(8,128)(2,1)S(1)}, bf16[256,768]{1,0:T(8,128)(2,1)S(1)}, u32[]{:S(2)}, u32[]{:S(2)}) collective-permute-start(bf16[256,768]{1,0:T(8,128)(2,1)S(1)} %bitcast.132), channel_id=1, source_target_pairs={{0,2},{1,3},{2,0},{3,1},{4,6},{5,7},{6,4},{7,5},{8,10},{9,11},{10,... | collective-permute-start | bytes 1179656 | tf_op jit(solution)/shard_map/ppermute | solution.py:56
  61.6 18.7 %collective-permute-start.2 = (bf16[256,768]{1,0:T(8,128)(2,1)S(1)}, bf16[256,768]{1,0:T(8,128)(2,1)S(1)}, u32[]{:S(2)}, u32[]{:S(2)}) collective-permute-start(bf16[256,768]{1,0:T(8,128)(2,1)S(1)} %bitcast.131), channel_id=1, source_target_pairs={{0,3},{1,0},{2,1},{3,2},{4,7},{5,4},{6,5},{7,6},{8,11},{9,8},{10,9... | collective-permute-start | bytes 1179656 | tf_op jit(solution)/shard_map/ppermute | solution.py:56
  87.4 162.5 %copy-start.6 = (pred[6,10]{0,1:T(8,128)(4,1)S(1)}, pred[6,10]{0,1:T(8,128)(4,1)}, u32[]{:S(2)}) copy-start(pred[6,10]{0,1:T(8,128)(4,1)} %copy.78) | copy-start | bytes 184
  87.5 162.6 %copy-start.8 = (s32[60]{0:T(128)S(1)}, s32[60]{0:T(128)}, u32[]{:S(2)}) copy-start(s32[60]{0:T(128)} %get-tuple-element.62) | copy-start | bytes 724
  87.5 162.6 %copy-start.9 = (s32[128]{0:T(128)S(1)}, s32[128]{0:T(128)}, u32[]{:S(2)}) copy-start(s32[128]{0:T(128)} %get-tuple-element.74) | copy-start | bytes 1540
  241.0 197.1 %all-to-all-start.2 = ((bf16[128,128,128]{2,1,0:T(8,128)(2,1)}), bf16[128,128,128]{2,1,0:T(8,128)(2,1)}, u32[]{:S(2)}, u32[]{:S(2)}) async-start(bf16[128,128,128]{2,1,0:T(8,128)(2,1)} %gather_fusion.2), calls=%async_computation.2 | async-start | bytes 8388608 | tf_op jit(solution)/shard_map/all_to_all | solution.py:113
  255.8 2.8 copy-start
  266.5 2.8 copy-start
  277.3 2.8 copy-start
  288.0 2.8 copy-start
  298.8 2.8 copy-start
  309.4 2.8 copy-start
  456.3 9.1 %copy-start.11 = (s32[48]{0:T(128)S(1)}, s32[48]{0:T(128)}, u32[]{:S(2)}) copy-start(s32[48]{0:T(128)} %copy-done.10) | copy-start | bytes 580
  456.3 9.1 %copy-start.13 = (s32[48]{0:T(128)S(1)}, s32[48]{0:T(128)}, u32[]{:S(2)}) copy-start(s32[48]{0:T(128)} %copy-done.12) | copy-start | bytes 580
  456.3 197.2 %all-to-all-start.3 = ((bf16[128,128,128]{2,1,0:T(8,128)(2,1)}), bf16[128,128,128]{2,1,0:T(8,128)(2,1)}, u32[]{:S(2)}, u32[]{:S(2)}) async-start(bf16[128,128,128]{2,1,0:T(8,128)(2,1)} %gather_fusion.5), calls=%async_computation.3 | async-start | bytes 8388608 | tf_op jit(solution)/shard_map/all_to_all | solution.py:136

commit v7 on v6

--- a/solution.py
+++ b/solution.py
@@ -83,6 +83,14 @@
     send_pick = jnp.sum(jnp.where(slot_match, item_ids[None, :], 0), axis=1) + item_count * (
         1 - jnp.any(slot_match, axis=1).astype(jnp.int32)
     )
+    key_send, group_ids = lax.optimization_barrier((by_index(key_items, send_pick), group_ids))
+    arrived_k = lax.all_to_all(key_send, "seq", split_axis=0, concat_axis=0, tiled=True)
+    value_send = by_index(value_items, send_pick)
+    arrived_k, value_send = lax.optimization_barrier((arrived_k, value_send))
+    arrived_v = lax.all_to_all(value_send, "seq", split_axis=0, concat_axis=0, tiled=True)
+    by_source = jnp.transpose(
+        group_ids.reshape(group_heads, seq_count, shard_blocks), (1, 0, 2)
+    ).reshape(seq_count, item_count)
     received_mask = (by_source == seq_index).astype(jnp.int32)
     recv_pos = (
         jnp.arange(seq_count, dtype=jnp.int32)[:, None] * slot_count
@@ -105,12 +113,6 @@
     )
     block_ids = jnp.tile(jnp.arange(all_blocks, dtype=jnp.int32), group_heads)
     block_of = jnp.sum(jnp.where(matches, block_ids[None, :], 0), axis=1)
-    arrived_k = lax.all_to_all(
-        by_index(key_items, send_pick), "seq", split_axis=0, concat_axis=0, tiled=True
-    )
-    value_send = by_index(value_items, send_pick)
-    arrived_k, value_send = lax.optimization_barrier((arrived_k, value_send))
-    arrived_v = lax.all_to_all(value_send, "seq", split_axis=0, concat_axis=0, tiled=True)
     key_grouped = by_index(arrived_k, source_row)
     value_grouped = by_index(arrived_v, source_row)
     positions = (block_of[:, None] * BLK + jnp.arange(BLK, dtype=jnp.int32)[None, :]).reshape(

time: 685 us -> 685 us (level)
  waiting for transfers between devices: 481 us -> 508 us
  other arithmetic: 55.7 us -> 39.2 us
  local copies, waits for them, and re-layouts: 51.1 us -> 40.9 us
    all_to_all x1, waiting for transfers between devices: 121 us -> 139 us  [shards(): lax.all_to_all(value_send, 'seq', split_axis=0, concat_axis=0, tiled=True)]
    all_to_all x1, waiting for transfers between devices: 3.69 us -> 16.1 us  [shards(): lax.all_to_all(query_key, 'fsdp', split_axis=1, concat_axis=0, tiled=True)]
    dynamic_update_slice x12, other arithmetic: 31.3 us -> 20.4 us  [shards(): lax.map(one_head, (key_grouped.reshape(group_heads, group_rows, head_dim)...]
  transfers between devices with their start and end apart: 7 -> 7, of which waited for: 6 -> 6; matrix products, arithmetic and copies ran while one was open for 13% -> 10% of each run, Pallas kernels for 0% -> 0%
where the time goes in v7:
time: 685 us; the launch traced here: 684 us
  waiting for transfers between devices  508 us (74%)
  starting transfers between devices  50.4 us (7%)
  local copies, waits for them, and re-layouts  40.9 us (6%)
  other arithmetic  39.2 us (6%)
  blocking collectives  23.6 us (3%)
  matrix products  21.4 us (3%)
    all_to_all x1, waiting for transfers between devices, shards(): lax.all_to_all(by_index(outputs, back_pick), 'seq', split_axis=0, concat_...  188 us
    all_to_all x1, waiting for transfers between devices, shards(): lax.all_to_all(key_send, 'seq', split_axis=0, concat_axis=0, tiled=True)  151 us
    all_to_all x1, waiting for transfers between devices, shards(): lax.all_to_all(value_send, 'seq', split_axis=0, concat_axis=0, tiled=True)  139 us
    all_to_all x1, blocking collectives, shards(): lax.all_to_all(jnp.swapaxes(own_output, 0, 1), 'fsdp', split_axis=0, conc...  23.6 us
    dynamic_update_slice x12, other arithmetic, shards(): lax.map(one_head, (key_grouped.reshape(group_heads, group_rows, head_dim)...  20.4 us
    gather x6, local copies, waits for them, and re-layouts, by_index(): return source_table[jnp.clip(row_index, 0, source_table.shape[0] - 1)]  19.8 us
    all_to_all x1, starting transfers between devices, shards(): lax.all_to_all(key_send, 'seq', split_axis=0, concat_axis=0, tiled=True)  18.9 us
    all_to_all x1, waiting for transfers between devices, shards(): lax.all_to_all(query_key, 'fsdp', split_axis=1, concat_axis=0, tiled=True)  16.1 us
  transfers between devices with their start and end apart: 7, of which 6 were waited for; matrix products, arithmetic and copies ran while one was open for 10% of the time, Pallas kernels for 0%

profile of v7, /device:TPU:70, one launch (start us, length us, event | category | flops | bytes accessed | tf_op | source)
XLA Modules:
  0.0 684.2 jit_solution(3121798839654760957)
XLA Ops:
  0.0 2.6 copy.60
  2.6 4.6 all-to-all-start
  11.8 16.1 %all-to-all-done = bf16[256,4,768]{0,2,1:T(8,128)(2,1)S(1)} async-done(((bf16[256,4,768]{0,2,1:T(8,128)(2,1)}), bf16[256,4,768]{0,2,1:T(8,128)(2,1)S(1)}, u32[]{:S(2)}, u32[]{:S(2)}) %all-to-all-start) | async-done | bytes 1572896 | tf_op jit(solution)/shard_map/all_to_all | solution.py:47
  31.0 3.1 gather_fusion
  34.1 18.9 %all-to-all-start.1 = ((bf16[128,128,128]{2,1,0:T(8,128)(2,1)}), bf16[128,128,128]{2,1,0:T(8,128)(2,1)}, u32[]{:S(2)}, u32[]{:S(2)}) async-start(bf16[128,128,128]{2,1,0:T(8,128)(2,1)} %gather_fusion), calls=%async_computation.1 | async-start | bytes 8388608 | tf_op jit(solution)/shard_map/all_to_all | solution.py:87
  56.7 2.5 collective-permute-start
  59.4 4.0 collective-permute-start.1
  63.5 2.5 collective-permute-start.2
  67.9 11.5 %collective-permute-done = bf16[256,768]{1,0:T(8,128)(2,1)S(1)} collective-permute-done((bf16[256,768]{1,0:T(8,128)(2,1)S(1)}, bf16[256,768]{1,0:T(8,128)(2,1)S(1)}, u32[]{:S(2)}, u32[]{:S(2)}) %collective-permute-start) | collective-permute-done | bytes 393248 | tf_op jit(solution)/shard_map/ppermute | solution.py:56
  79.4 2.7 collective-permute-done.2
  87.5 3.1 gather_fusion.2
  90.7 150.5 %all-to-all-done.1 = bf16[128,128,128]{2,1,0:T(8,128)(2,1)} async-done(((bf16[128,128,128]{2,1,0:T(8,128)(2,1)}), bf16[128,128,128]{2,1,0:T(8,128)(2,1)}, u32[]{:S(2)}, u32[]{:S(2)}) %all-to-all-start.1) | async-done | bytes 4194336 | tf_op jit(solution)/shard_map/all_to_all | solution.py:87
  241.2 8.9 %all-to-all-start.2 = ((bf16[128,128,128]{2,1,0:T(8,128)(2,1)}), bf16[128,128,128]{2,1,0:T(8,128)(2,1)}, u32[]{:S(2)}, u32[]{:S(2)}) async-start(bf16[128,128,128]{2,1,0:T(8,128)(2,1)} %gather_fusion.2), calls=%async_computation.2 | async-start | bytes 8388608 | tf_op jit(solution)/shard_map/all_to_all | solution.py:90
  250.2 3.1 gather_fusion.3
  253.3 46.0 %while.12 = (s32[]{:T(128)}, bf16[6,1280,1280]{1,2,0:T(8,128)(2,1)}, f32[6,1280,1]{1,0,2:T(8,128)S(1)}, pred[6,1280]{1,0:T(8,128)(4,1)S(1)}, s32[6,1280]{1,0:T(8...) while((s32[]{:T(128)}, bf16[6,1280,1280]{1,2,0:T(8,128)(2,1)}, ...), condition=%wide.region_12.13_spmd, body=%wide.region_9.12_spmd.sunk | while | flops 444005120 | bytes 23367272 | solution.py:127
  255.1 3.4 fusion.31
  258.5 2.3 fusion.32
  262.7 3.4 fusion.31
  266.1 2.3 fusion.32
  270.4 3.4 fusion.31
  278.1 3.4 fusion.31
  285.8 3.4 fusion.31
  293.5 3.4 fusion.31
  299.3 138.9 %all-to-all-done.2 = bf16[128,128,128]{2,1,0:T(8,128)(2,1)} async-done(((bf16[128,128,128]{2,1,0:T(8,128)(2,1)}), bf16[128,128,128]{2,1,0:T(8,128)(2,1)}, u32[]{:S(2)}, u32[]{:S(2)}) %all-to-all-start.2) | async-done | bytes 4194336 | tf_op jit(solution)/shard_map/all_to_all | solution.py:90
  438.2 4.4 gather_fusion.4
  442.6 11.0 %divide_convert_fusion = bf16[6,1280,128]{2,1,0:T(8,128)(2,1)S(1)} fusion(bf16[6,1280,1280]{1,2,0:T(8,128)(2,1)} %get-tuple-element.49, bf16[6,1280,128]{2,1,0:T(8,128)(2,1)} %bitcast.118, f32[6,1280]{1,0:T(8,128)S(1)} %bitcast.134), kind=kOutput, calls=%fused_computation.22 | convolution fusion | flops 2518548480 | bytes 23623680 | tf_op jit(solution)/shard_map/hqk,hkd->hqd/dot_general | solution.py:136
  453.6 3.1 gather_fusion.5
  456.6 8.9 %all-to-all-start.3 = ((bf16[128,128,128]{2,1,0:T(8,128)(2,1)}), bf16[128,128,128]{2,1,0:T(8,128)(2,1)}, u32[]{:S(2)}, u32[]{:S(2)}) async-start(bf16[128,128,128]{2,1,0:T(8,128)(2,1)} %gather_fusion.5), calls=%async_computation.3 | async-start | bytes 8388608 | tf_op jit(solution)/shard_map/all_to_all | solution.py:138
  465.6 188.1 %all-to-all-done.3 = bf16[128,128,128]{2,1,0:T(8,128)(2,1)} async-done(((bf16[128,128,128]{2,1,0:T(8,128)(2,1)}), bf16[128,128,128]{2,1,0:T(8,128)(2,1)}, u32[]{:S(2)}, u32[]{:S(2)}) %all-to-all-start.3) | async-done | bytes 4194336 | tf_op jit(solution)/shard_map/all_to_all | solution.py:138
  653.7 3.0 gather_fusion.6
  656.9 23.6 %all_to_all.39 = bf16[4,6,2,128,128]{4,3,2,1,0:T(8,128)(2,1)S(1)} all-to-all(bf16[4,6,2,128,128]{4,3,2,1,0:T(8,128)(2,1)S(1)} %copy.77), channel_id=1, replica_groups=mesh['seq'=128,'fsdp'=4] {'fsdp'}, dimensions={0} | all-to-all | bytes 3145728 | tf_op jit(solution)/shard_map/all_to_all | solution.py:144
  681.6 2.6 reshape.391
  (113 shorter events, 40.6 us)
Async XLA Ops:
  0.0 7.2 %copy-start = (s32[24,1024]{1,0:T(8,128)S(1)}, s32[24,1024]{1,0:T(8,128)}, u32[]{:S(2)}) copy-start(s32[24,1024]{1,0:T(8,128)} %param.7) | copy-start | bytes 294916
  2.6 7.2 %copy-start.3 = (bf16[256,3072]{1,0:T(8,128)(2,1)S(1)}, bf16[256,3072]{1,0:T(8,128)(2,1)}, u32[]{:S(2)}) copy-start(bf16[256,3072]{1,0:T(8,128)(2,1)} %param.6) | copy-start | bytes 4718596
  2.6 25.3 %all-to-all-start = ((bf16[256,4,768]{0,2,1:T(8,128)(2,1)}), bf16[256,4,768]{0,2,1:T(8,128)(2,1)S(1)}, u32[]{:S(2)}, u32[]{:S(2)}) async-start(bf16[256,4,768]{0,2,1:T(8,128)(2,1)} %bitcast.4), calls=%async_computation | async-start | bytes 3145728 | tf_op jit(solution)/shard_map/all_to_all | solution.py:47
  34.1 207.1 %all-to-all-start.1 = ((bf16[128,128,128]{2,1,0:T(8,128)(2,1)}), bf16[128,128,128]{2,1,0:T(8,128)(2,1)}, u32[]{:S(2)}, u32[]{:S(2)}) async-start(bf16[128,128,128]{2,1,0:T(8,128)(2,1)} %gather_fusion), calls=%async_computation.1 | async-start | bytes 8388608 | tf_op jit(solution)/shard_map/all_to_all | solution.py:87
  53.0 3.4 copy-start.2
  56.7 22.7 %collective-permute-start = (bf16[256,768]{1,0:T(8,128)(2,1)S(1)}, bf16[256,768]{1,0:T(8,128)(2,1)S(1)}, u32[]{:S(2)}, u32[]{:S(2)}) collective-permute-start(bf16[256,768]{1,0:T(8,128)(2,1)S(1)} %bitcast.124), channel_id=1, source_target_pairs={{0,1},{1,2},{2,3},{3,0},{4,5},{5,6},{6,7},{7,4},{8,9},{9,10},{10,1... | collective-permute-start | bytes 1179656 | tf_op jit(solution)/shard_map/ppermute | solution.py:56
  59.4 20.0 %collective-permute-start.1 = (bf16[256,768]{1,0:T(8,128)(2,1)S(1)}, bf16[256,768]{1,0:T(8,128)(2,1)S(1)}, u32[]{:S(2)}, u32[]{:S(2)}) collective-permute-start(bf16[256,768]{1,0:T(8,128)(2,1)S(1)} %bitcast.125), channel_id=1, source_target_pairs={{0,2},{1,3},{2,0},{3,1},{4,6},{5,7},{6,4},{7,5},{8,10},{9,11},{10,... | collective-permute-start | bytes 1179656 | tf_op jit(solution)/shard_map/ppermute | solution.py:56
  63.5 18.6 %collective-permute-start.2 = (bf16[256,768]{1,0:T(8,128)(2,1)S(1)}, bf16[256,768]{1,0:T(8,128)(2,1)S(1)}, u32[]{:S(2)}, u32[]{:S(2)}) collective-permute-start(bf16[256,768]{1,0:T(8,128)(2,1)S(1)} %bitcast.126), channel_id=1, source_target_pairs={{0,3},{1,0},{2,1},{3,2},{4,7},{5,4},{6,5},{7,6},{8,11},{9,8},{10,9... | collective-permute-start | bytes 1179656 | tf_op jit(solution)/shard_map/ppermute | solution.py:56
  82.1 0.7 copy-start.4
  241.2 197.1 %all-to-all-start.2 = ((bf16[128,128,128]{2,1,0:T(8,128)(2,1)}), bf16[128,128,128]{2,1,0:T(8,128)(2,1)}, u32[]{:S(2)}, u32[]{:S(2)}) async-start(bf16[128,128,128]{2,1,0:T(8,128)(2,1)} %gather_fusion.2), calls=%async_computation.2 | async-start | bytes 8388608 | tf_op jit(solution)/shard_map/all_to_all | solution.py:90
  456.6 197.1 %all-to-all-start.3 = ((bf16[128,128,128]{2,1,0:T(8,128)(2,1)}), bf16[128,128,128]{2,1,0:T(8,128)(2,1)}, u32[]{:S(2)}, u32[]{:S(2)}) async-start(bf16[128,128,128]{2,1,0:T(8,128)(2,1)} %gather_fusion.5), calls=%async_computation.3 | async-start | bytes 8388608 | tf_op jit(solution)/shard_map/all_to_all | solution.py:138
  680.5 3.7 copy-start.1

commit v8 on v7

--- a/solution.py
+++ b/solution.py
@@ -138,14 +138,11 @@
     returned = lax.all_to_all(
         by_index(outputs, back_pick), "seq", split_axis=0, concat_axis=0, tiled=True
     )
-    own_output = by_index(returned, own_pos).reshape(
-        group_heads, group_count, own_blocks, BLK, head_dim
-    )
-    gathered = lax.all_to_all(
-        jnp.swapaxes(own_output, 0, 1), "fsdp", split_axis=0, concat_axis=0, tiled=True
-    )
-    token_major = jnp.transpose(gathered, (2, 3, 0, 1, 4))
-    return token_major.reshape(tok_rows, heads_all * head_dim)
+    own_output = by_index(returned, own_pos)
+    token_major = jnp.transpose(
+        own_output.reshape(group_heads, shard_blocks, BLK, head_dim), (1, 2, 0, 3)
+    ).reshape(shard_blocks * BLK, group_heads * head_dim)
+    return lax.all_to_all(token_major, "fsdp", split_axis=0, concat_axis=1, tiled=True)
 
 
 def solution(mesh):

time: 685 us -> 685 us (level)
  no operation moved by 1% of the time
where the time goes in v8:
time: 685 us; the launch traced here: 684 us
  waiting for transfers between devices  508 us (74%)
  starting transfers between devices  50.4 us (7%)
  local copies, waits for them, and re-layouts  41 us (6%)
  other arithmetic  39.2 us (6%)
  blocking collectives  23.7 us (3%)
  matrix products  21.4 us (3%)
    all_to_all x1, waiting for transfers between devices, shards(): lax.all_to_all(by_index(outputs, back_pick), 'seq', split_axis=0, concat_...  188 us
    all_to_all x1, waiting for transfers between devices, shards(): lax.all_to_all(key_send, 'seq', split_axis=0, concat_axis=0, tiled=True)  151 us
    all_to_all x1, waiting for transfers between devices, shards(): lax.all_to_all(value_send, 'seq', split_axis=0, concat_axis=0, tiled=True)  139 us
    all_to_all x1, blocking collectives, shards(): lax.all_to_all(token_major, 'fsdp', split_axis=0, concat_axis=1, tiled=True)  23.7 us
    dynamic_update_slice x12, other arithmetic, shards(): lax.map(one_head, (key_grouped.reshape(group_heads, group_rows, head_dim)...  20.4 us
    gather x6, local copies, waits for them, and re-layouts, by_index(): return source_table[jnp.clip(row_index, 0, source_table.shape[0] - 1)]  19.8 us
    all_to_all x1, starting transfers between devices, shards(): lax.all_to_all(key_send, 'seq', split_axis=0, concat_axis=0, tiled=True)  18.9 us
    all_to_all x1, waiting for transfers between devices, shards(): lax.all_to_all(query_key, 'fsdp', split_axis=1, concat_axis=0, tiled=True)  16.1 us
  transfers between devices with their start and end apart: 7, of which 6 were waited for; matrix products, arithmetic and copies ran while one was open for 10% of the time, Pallas kernels for 0%

profile of v8, /device:TPU:70, one launch (start us, length us, event | category | flops | bytes accessed | tf_op | source)
XLA Modules:
  0.0 684.4 jit_solution(7118811950507053545)
XLA Ops:
  0.0 2.6 copy.59
  2.6 4.6 all-to-all-start
  11.8 16.1 %all-to-all-done = bf16[256,4,768]{0,2,1:T(8,128)(2,1)S(1)} async-done(((bf16[256,4,768]{0,2,1:T(8,128)(2,1)}), bf16[256,4,768]{0,2,1:T(8,128)(2,1)S(1)}, u32[]{:S(2)}, u32[]{:S(2)}) %all-to-all-start) | async-done | bytes 1572896 | tf_op jit(solution)/shard_map/all_to_all | solution.py:47
  31.0 3.1 gather_fusion
  34.1 18.9 %all-to-all-start.1 = ((bf16[128,128,128]{2,1,0:T(8,128)(2,1)}), bf16[128,128,128]{2,1,0:T(8,128)(2,1)}, u32[]{:S(2)}, u32[]{:S(2)}) async-start(bf16[128,128,128]{2,1,0:T(8,128)(2,1)} %gather_fusion), calls=%async_computation.1 | async-start | bytes 8388608 | tf_op jit(solution)/shard_map/all_to_all | solution.py:87
  56.7 2.5 collective-permute-start
  59.4 4.0 collective-permute-start.1
  63.5 2.5 collective-permute-start.2
  67.9 11.5 %collective-permute-done = bf16[256,768]{1,0:T(8,128)(2,1)S(1)} collective-permute-done((bf16[256,768]{1,0:T(8,128)(2,1)S(1)}, bf16[256,768]{1,0:T(8,128)(2,1)S(1)}, u32[]{:S(2)}, u32[]{:S(2)}) %collective-permute-start) | collective-permute-done | bytes 393248 | tf_op jit(solution)/shard_map/ppermute | solution.py:56
  79.4 2.7 collective-permute-done.2
  87.5 3.1 gather_fusion.2
  90.7 150.5 %all-to-all-done.1 = bf16[128,128,128]{2,1,0:T(8,128)(2,1)} async-done(((bf16[128,128,128]{2,1,0:T(8,128)(2,1)}), bf16[128,128,128]{2,1,0:T(8,128)(2,1)}, u32[]{:S(2)}, u32[]{:S(2)}) %all-to-all-start.1) | async-done | bytes 4194336 | tf_op jit(solution)/shard_map/all_to_all | solution.py:87
  241.2 8.9 %all-to-all-start.2 = ((bf16[128,128,128]{2,1,0:T(8,128)(2,1)}), bf16[128,128,128]{2,1,0:T(8,128)(2,1)}, u32[]{:S(2)}, u32[]{:S(2)}) async-start(bf16[128,128,128]{2,1,0:T(8,128)(2,1)} %gather_fusion.2), calls=%async_computation.2 | async-start | bytes 8388608 | tf_op jit(solution)/shard_map/all_to_all | solution.py:90
  250.2 3.1 gather_fusion.3
  253.3 46.0 %while.12 = (s32[]{:T(128)}, bf16[6,1280,1280]{1,2,0:T(8,128)(2,1)}, f32[6,1280,1]{1,0,2:T(8,128)S(1)}, pred[6,1280]{1,0:T(8,128)(4,1)S(1)}, s32[6,1280]{1,0:T(8...) while((s32[]{:T(128)}, bf16[6,1280,1280]{1,2,0:T(8,128)(2,1)}, ...), condition=%wide.region_12.13_spmd, body=%wide.region_9.12_spmd.sunk | while | flops 444005120 | bytes 23367272 | solution.py:127
  255.1 3.4 fusion.31
  258.5 2.3 fusion.32
  262.7 3.4 fusion.31
  266.1 2.3 fusion.32
  270.4 3.4 fusion.31
  278.1 3.4 fusion.31
  281.5 2.3 fusion.32
  285.8 3.4 fusion.31
  293.5 3.4 fusion.31
  299.3 138.9 %all-to-all-done.2 = bf16[128,128,128]{2,1,0:T(8,128)(2,1)} async-done(((bf16[128,128,128]{2,1,0:T(8,128)(2,1)}), bf16[128,128,128]{2,1,0:T(8,128)(2,1)}, u32[]{:S(2)}, u32[]{:S(2)}) %all-to-all-start.2) | async-done | bytes 4194336 | tf_op jit(solution)/shard_map/all_to_all | solution.py:90
  438.2 4.4 gather_fusion.4
  442.6 11.0 %divide_convert_fusion = bf16[6,1280,128]{2,1,0:T(8,128)(2,1)S(1)} fusion(bf16[6,1280,1280]{1,2,0:T(8,128)(2,1)} %get-tuple-element.49, bf16[6,1280,128]{2,1,0:T(8,128)(2,1)} %bitcast.124, f32[6,1280]{1,0:T(8,128)S(1)} %bitcast.140), kind=kOutput, calls=%fused_computation.22 | convolution fusion | flops 2518548480 | bytes 23623680 | tf_op jit(solution)/shard_map/hqk,hkd->hqd/dot_general | solution.py:136
  453.6 3.1 gather_fusion.5
  456.6 8.9 %all-to-all-start.3 = ((bf16[128,128,128]{2,1,0:T(8,128)(2,1)}), bf16[128,128,128]{2,1,0:T(8,128)(2,1)}, u32[]{:S(2)}, u32[]{:S(2)}) async-start(bf16[128,128,128]{2,1,0:T(8,128)(2,1)} %gather_fusion.5), calls=%async_computation.3 | async-start | bytes 8388608 | tf_op jit(solution)/shard_map/all_to_all | solution.py:138
  465.6 188.1 %all-to-all-done.3 = bf16[128,128,128]{2,1,0:T(8,128)(2,1)} async-done(((bf16[128,128,128]{2,1,0:T(8,128)(2,1)}), bf16[128,128,128]{2,1,0:T(8,128)(2,1)}, u32[]{:S(2)}, u32[]{:S(2)}) %all-to-all-start.3) | async-done | bytes 4194336 | tf_op jit(solution)/shard_map/all_to_all | solution.py:138
  653.7 3.0 gather_fusion.6
  659.0 23.7 %all_to_all.53 = bf16[4,256,768]{1,2,0:T(8,128)(2,1)S(1)} all-to-all(bf16[4,256,768]{1,2,0:T(8,128)(2,1)S(1)} %copy.77), channel_id=1, replica_groups=mesh['seq'=128,'fsdp'=4] {'fsdp'}, dimensions={0} | all-to-all | bytes 3145728 | tf_op jit(solution)/shard_map/all_to_all | solution.py:145
  (114 shorter events, 41.1 us)
Async XLA Ops:
  0.0 7.2 %copy-start = (s32[24,1024]{1,0:T(8,128)S(1)}, s32[24,1024]{1,0:T(8,128)}, u32[]{:S(2)}) copy-start(s32[24,1024]{1,0:T(8,128)} %param.7) | copy-start | bytes 294916
  2.6 7.2 %copy-start.3 = (bf16[256,3072]{1,0:T(8,128)(2,1)S(1)}, bf16[256,3072]{1,0:T(8,128)(2,1)}, u32[]{:S(2)}) copy-start(bf16[256,3072]{1,0:T(8,128)(2,1)} %param.6) | copy-start | bytes 4718596
  2.6 25.3 %all-to-all-start = ((bf16[256,4,768]{0,2,1:T(8,128)(2,1)}), bf16[256,4,768]{0,2,1:T(8,128)(2,1)S(1)}, u32[]{:S(2)}, u32[]{:S(2)}) async-start(bf16[256,4,768]{0,2,1:T(8,128)(2,1)} %bitcast.4), calls=%async_computation | async-start | bytes 3145728 | tf_op jit(solution)/shard_map/all_to_all | solution.py:47
  34.1 207.1 %all-to-all-start.1 = ((bf16[128,128,128]{2,1,0:T(8,128)(2,1)}), bf16[128,128,128]{2,1,0:T(8,128)(2,1)}, u32[]{:S(2)}, u32[]{:S(2)}) async-start(bf16[128,128,128]{2,1,0:T(8,128)(2,1)} %gather_fusion), calls=%async_computation.1 | async-start | bytes 8388608 | tf_op jit(solution)/shard_map/all_to_all | solution.py:87
  53.0 3.4 copy-start.2
  56.7 22.7 %collective-permute-start = (bf16[256,768]{1,0:T(8,128)(2,1)S(1)}, bf16[256,768]{1,0:T(8,128)(2,1)S(1)}, u32[]{:S(2)}, u32[]{:S(2)}) collective-permute-start(bf16[256,768]{1,0:T(8,128)(2,1)S(1)} %bitcast.130), channel_id=1, source_target_pairs={{0,1},{1,2},{2,3},{3,0},{4,5},{5,6},{6,7},{7,4},{8,9},{9,10},{10,1... | collective-permute-start | bytes 1179656 | tf_op jit(solution)/shard_map/ppermute | solution.py:56
  59.4 20.0 %collective-permute-start.1 = (bf16[256,768]{1,0:T(8,128)(2,1)S(1)}, bf16[256,768]{1,0:T(8,128)(2,1)S(1)}, u32[]{:S(2)}, u32[]{:S(2)}) collective-permute-start(bf16[256,768]{1,0:T(8,128)(2,1)S(1)} %bitcast.131), channel_id=1, source_target_pairs={{0,2},{1,3},{2,0},{3,1},{4,6},{5,7},{6,4},{7,5},{8,10},{9,11},{10,... | collective-permute-start | bytes 1179656 | tf_op jit(solution)/shard_map/ppermute | solution.py:56
  63.5 18.6 %collective-permute-start.2 = (bf16[256,768]{1,0:T(8,128)(2,1)S(1)}, bf16[256,768]{1,0:T(8,128)(2,1)S(1)}, u32[]{:S(2)}, u32[]{:S(2)}) collective-permute-start(bf16[256,768]{1,0:T(8,128)(2,1)S(1)} %bitcast.132), channel_id=1, source_target_pairs={{0,3},{1,0},{2,1},{3,2},{4,7},{5,4},{6,5},{7,6},{8,11},{9,8},{10,9... | collective-permute-start | bytes 1179656 | tf_op jit(solution)/shard_map/ppermute | solution.py:56
  82.1 0.7 copy-start.4
  241.2 197.1 %all-to-all-start.2 = ((bf16[128,128,128]{2,1,0:T(8,128)(2,1)}), bf16[128,128,128]{2,1,0:T(8,128)(2,1)}, u32[]{:S(2)}, u32[]{:S(2)}) async-start(bf16[128,128,128]{2,1,0:T(8,128)(2,1)} %gather_fusion.2), calls=%async_computation.2 | async-start | bytes 8388608 | tf_op jit(solution)/shard_map/all_to_all | solution.py:90
  456.6 197.1 %all-to-all-start.3 = ((bf16[128,128,128]{2,1,0:T(8,128)(2,1)}), bf16[128,128,128]{2,1,0:T(8,128)(2,1)}, u32[]{:S(2)}, u32[]{:S(2)}) async-start(bf16[128,128,128]{2,1,0:T(8,128)(2,1)} %gather_fusion.5), calls=%async_computation.3 | async-start | bytes 8388608 | tf_op jit(solution)/shard_map/all_to_all | solution.py:138
  659.0 25.4 %copy-start.1 = (s32[24,1024]{1,0:T(8,128)S(1)}, s32[24,1024]{1,0:T(8,128)}, u32[]{:S(2)}) copy-start(s32[24,1024]{1,0:T(8,128)} %param.7) | copy-start | bytes 294916
